TPU v7x, 512 devices: a whole 4x4x16 slice. The times are simulated.
512 devices in a mesh: lat: 128 (over x, z, core), lev: 4 (over y).
Axes of the slice: x: 4, y: 4, z: 16, core: 2. Of those that a mesh axis runs over, the one named last changes fastest.
Arguments:
- fields: float32 [2, 640, 8, 2560], P(None, 'lat', 'lev'), may hold values from -6 to 6
- dep_row: int32 [640, 8, 2560], P('lat', 'lev'), may hold values from -2 to 2
- dep_col: int32 [640, 8, 2560], P('lat', 'lev'), may hold values from -4 to 4
- legendre: bfloat16 [384, 640, 384], P('lat'), may hold values from -0.25 to 0.25
- lat_weights: float32 [640], replicated, may hold values from 0.3 to 1.7
- to_modes: float32 [8, 8], replicated, may hold values from -2 to 2
- from_modes: float32 [8, 8], replicated, may hold values from -2 to 2
- mode_rates: float32 [8], replicated, may hold values from 0.1 to 10
Outputs:
- updated: float32 [2, 640, 8, 2560], P(None, 'lat', 'lev')
Inputs may be any that keep to these rules, and one draw needn't show every extreme that they name: `dep_row`: departure rows lie within two latitudes of the arrival row. `dep_col`: departure columns lie within four longitudes of the arrival column.
All inputs are finite; a program needn't handle non-finite values.
Results may differ from a plain program's by a relative error of at most 0.0003.
Values sent between devices are 32-bit elements; how exact they have to be, the bound alone decides.
No kernel may reach another device: no remote copies, remote signals or barrier semaphores. Data moves between devices by JAX's collectives and lax.ppermute only.
A program may use at most 64 MiB of HBM per device.

v0:
```python
import math

import jax
import jax.numpy as jnp
import numpy as np
from jax import lax
from jax.experimental import pallas as pl
from jax.experimental.pallas import tpu as pltpu
from jax.sharding import Mesh
from jax.sharding import PartitionSpec as P

stencil_weights = (-0.0625, 0.5625, 0.5625, -0.0625)
stiffness = 4.0
highest = lax.Precision.HIGHEST

LAT = ("lo", "lc")


def with_halo(block, count, width):
    forward = [(i, i + 1) for i in range(count - 1)]
    backward = [(target, source) for source, target in forward]
    low = lax.ppermute(lax.slice_in_dim(block, block.shape[1] - width, None, axis=1), LAT, forward)
    high = lax.ppermute(lax.slice_in_dim(block, 0, width, axis=1), LAT, backward)
    return jnp.concatenate([low, block, high], axis=1)


def tap_weight(dep, shift):
    k = shift + 1 - dep
    outer = jnp.where((k == 0) | (k == 3), jnp.float32(stencil_weights[0]), jnp.float32(0.0))
    return jnp.where((k == 1) | (k == 2), jnp.float32(stencil_weights[1]), outer)


def departure_interp(padded, dep_row, dep_col, row_offset):
    npoint = dep_row.shape[1]
    col_shifts = range(-5, 7)
    col_weights = [tap_weight(dep_col, shift)[:, None] for shift in col_shifts]
    rolled = [jnp.roll(padded, -shift, axis=3) for shift in col_shifts]
    result = None
    for row_shift in range(-3, 5):
        first = row_offset + row_shift
        inner = None
        for weight, shifted in zip(col_weights, rolled):
            term = weight * lax.slice_in_dim(shifted, first, first + npoint, axis=2)
            inner = term if inner is None else inner + term
        term = tap_weight(dep_row, row_shift)[:, None] * inner
        result = term if result is None else result + term
    return result


def advect_kernel(padded_ref, row_ref, col_ref, out_ref, weight_ref):
    nfield = padded_ref.shape[1]
    npoint, nlon = row_ref.shape[1], row_ref.shape[2]
    dep_col = col_ref[0]
    for index, shift in enumerate(range(-5, 7)):
        weight_ref[index] = tap_weight(dep_col, shift)
    dep_row = row_ref[0]
    for field in range(nfield):
        result = None
        for row_shift in range(-3, 5):
            first = 4 + row_shift
            rows = padded_ref[0, field, first : first + npoint, :]
            inner = None
            for index, shift in enumerate(range(-5, 7)):
                rolled = pltpu.roll(rows, (-shift) % nlon, 1) if shift % nlon else rows
                term = weight_ref[index] * rolled
                inner = term if inner is None else inner + term
            term = tap_weight(dep_row, row_shift) * inner
            result = term if result is None else result + term
        out_ref[0, field] = result


def advect_kernel_call(padded, dep_row, dep_col, row_offset, interpret=False):
    nlev, nfield, nrow, nlon = padded.shape
    npoint = dep_row.shape[1]
    tall = -(-npoint // 8) * 8
    padded = jnp.pad(padded, ((0, 0), (0, 0), (0, tall + 8 - nrow), (0, 0)))
    dep_row = jnp.pad(dep_row, ((0, 0), (0, tall - npoint), (0, 0)))
    dep_col = jnp.pad(dep_col, ((0, 0), (0, tall - npoint), (0, 0)))
    out = pl.pallas_call(
        advect_kernel,
        grid=(nlev,),
        in_specs=[
            pl.BlockSpec((1, nfield, tall + 8, nlon), lambda l: (l, 0, 0, 0)),
            pl.BlockSpec((1, tall, nlon), lambda l: (l, 0, 0)),
            pl.BlockSpec((1, tall, nlon), lambda l: (l, 0, 0)),
        ],
        out_specs=pl.BlockSpec((1, nfield, tall, nlon), lambda l: (l, 0, 0, 0)),
        out_shape=jax.ShapeDtypeStruct((nlev, nfield, tall, nlon), jnp.float32),
        scratch_shapes=[pltpu.VMEM((12, tall, nlon), jnp.float32)],
        interpret=interpret,
    )(padded, dep_row, dep_col)
    return out[:, :, :npoint]


def split_factor(n):
    for b in range(int(math.isqrt(n)), 0, -1):
        if n % b == 0:
            return b
    return 1


def fourier_tables(nlon, cut_off):
    inner = split_factor(nlon)
    outer = nlon // inner
    wave = jnp.arange(cut_off, dtype=jnp.int32)[None, :]
    scale = jnp.float32(2.0 * math.pi / nlon)
    coarse = (jnp.arange(outer, dtype=jnp.int32)[:, None] * inner * wave % nlon).astype(jnp.float32) * scale
    fine = (jnp.arange(inner, dtype=jnp.int32)[:, None] * wave % nlon).astype(jnp.float32) * scale
    cos_c, sin_c = jnp.cos(coarse)[:, None, :], jnp.sin(coarse)[:, None, :]
    cos_f, sin_f = jnp.cos(fine)[None, :, :], jnp.sin(fine)[None, :, :]
    cosine = (cos_c * cos_f - sin_c * sin_f).reshape(nlon, cut_off)
    sine_part = (sin_c * cos_f + cos_c * sin_f).reshape(nlon, cut_off)
    forward = jnp.stack([cosine, -sine_part], 0) / jnp.float32(nlon)
    doubling = jnp.where(wave == 0, jnp.float32(1.0), jnp.float32(2.0))
    backward = jnp.stack([cosine * doubling, -sine_part * doubling], 0)
    return (forward, backward)


def triangle_mask(wave_first, wave_count, cut_off):
    wave = wave_first + jnp.arange(wave_count, dtype=jnp.int32)
    degree = jnp.arange(cut_off, dtype=jnp.int32)
    return (degree[None, :] >= wave[:, None]).astype(jnp.float32)


def damping(rates, degree_count, cut_off):
    degree = jnp.arange(degree_count, dtype=jnp.int32).astype(jnp.float32)
    degree_term = degree * (degree + 1.0) / jnp.float32(cut_off * (cut_off + 1))
    return 1.0 / (1.0 + stiffness * rates[:, None] * degree_term[None, :])


def make_per_device(n_lo, n_lc, n_lev):
    def per_device(fields, dep_row, dep_col, legendre, lat_weights, to_modes, from_modes, mode_rates):
        nfield, npoint, lev_dev, nlon = fields.shape
        wave_dev, nlat, cut_off = legendre.shape
        padded = with_halo(fields, n_lo * n_lc, 4)
        advected = advect_kernel_call(
            jnp.transpose(padded, (2, 0, 1, 3)),
            jnp.transpose(dep_row, (1, 0, 2)),
            jnp.transpose(dep_col, (1, 0, 2)),
            4,
        )
        forward, backward = fourier_tables(nlon, cut_off)
        nr = forward.shape[0]
        split = (n_lo, n_lc, wave_dev)
        coeffs = jnp.einsum("lfpj,rjm->mfrlp", advected, forward, precision=highest)
        coeffs = coeffs.reshape(*split, nfield, nr, lev_dev, npoint)
        coeffs = jnp.transpose(coeffs, (0, 1, 3, 4, 2, 5, 6))
        coeffs = coeffs.reshape(n_lo, n_lc * nfield * nr, wave_dev, 1, lev_dev, npoint)
        staged = lax.all_to_all(coeffs, ("lc", "lev"), split_axis=1, concat_axis=3, tiled=True)
        staged = staged.reshape(n_lo, 1, wave_dev, n_lc, n_lev, lev_dev, npoint)
        staged = lax.all_to_all(staged, "lo", split_axis=0, concat_axis=1, tiled=True)
        by_wave = staged.reshape(n_lo, wave_dev, n_lc, n_lev * lev_dev, npoint)
        wave_first = lax.axis_index(LAT) * wave_dev
        basis = legendre.astype(jnp.float32) * triangle_mask(wave_first, wave_dev, cut_off)[:, None, :]
        basis = basis.reshape(wave_dev, n_lo, n_lc, npoint, cut_off)
        weights = lat_weights.reshape(n_lo, 1, n_lc, 1, npoint)
        spectrum = jnp.einsum("awblp,wabpn->lwn", by_wave * weights, basis, precision=highest)
        modal = jnp.einsum("kl,lmn->kmn", to_modes, spectrum, precision=highest)
        scaled = modal * damping(mode_rates, cut_off, cut_off)[:, None, :]
        solved = jnp.einsum("lk,kmn->lmn", from_modes, scaled, precision=highest)
        gridded = jnp.einsum("lwn,wabpn->awblp", solved, basis, precision=highest)
        staged = gridded.reshape(n_lo, 1, wave_dev, n_lc * n_lev, 1, lev_dev, npoint)
        staged = lax.all_to_all(staged, "lo", split_axis=0, concat_axis=1, tiled=True)
        staged = lax.all_to_all(staged, ("lc", "lev"), split_axis=3, concat_axis=4, tiled=True)
        by_lat = staged.reshape(n_lo, wave_dev, n_lc, nfield, nr, lev_dev, npoint)
        by_lat = jnp.transpose(by_lat, (3, 4, 5, 6, 0, 2, 1)).reshape(nfield, nr, lev_dev, npoint, cut_off)
        return jnp.einsum("frlpm,rjm->fplj", by_lat, backward, precision=highest)

    return per_device


def solution(mesh):
    n_lat = mesh.shape["lat"]
    n_lev = mesh.shape["lev"]
    n_lc = 2 if n_lat % 2 == 0 else 1
    n_lo = n_lat // n_lc
    devices = np.asarray(mesh.devices).reshape(n_lo, n_lc, n_lev)
    staged_mesh = Mesh(devices, ("lo", "lc", "lev"))
    return jax.shard_map(
        make_per_device(n_lo, n_lc, n_lev),
        mesh=staged_mesh,
        in_specs=(
            P(None, LAT, "lev", None),
            P(LAT, "lev", None),
            P(LAT, "lev", None),
            P(LAT, None, None),
            P(),
            P(),
            P(),
            P(),
        ),
        out_specs=P(None, LAT, "lev", None),
        check_vma=False,
    )
```

profile of v0, /device:TPU:1, one launch (start us, length us, event | category | flops | bytes accessed | tf_op | source)
XLA Modules:
  0.0 164.9 jit_solution(16364301043634757731)
XLA Ops:
  0.0 1.0 copy.51
  1.0 0.8 fusion.48
  1.8 4.9 %collective-permute-start = (f32[2,4,2,2560]{3,1,0,2:T(4,128)}, f32[2,4,2,2560]{3,1,0,2:T(4,128)S(1)}, u32[]{:S(2)}, u32[]{:S(2)}) collective-permute-start(f32[2,4,2,2560]{3,1,0,2:T(4,128)} %get-tuple-element.5), channel_id=1, source_target_pairs={{0,4},{4,8},{8,12},{12,16},{16,20},{20,24},{24,28},{28,32},{32,36}... | collective-permute-start | bytes 491528 | tf_op jit(solution)/shard_map/ppermute | solution.py:22
  6.7 5.1 %collective-permute-start.1 = (f32[2,4,2,2560]{3,1,0,2:T(4,128)}, f32[2,4,2,2560]{3,1,0,2:T(4,128)}, u32[]{:S(2)}, u32[]{:S(2)}) collective-permute-start(f32[2,4,2,2560]{3,1,0,2:T(4,128)} %get-tuple-element.6), channel_id=1, source_target_pairs={{4,0},{8,4},{12,8},{16,12},{20,16},{24,20},{28,24},{32,28},{36,32}... | collective-permute-start | bytes 491528 | tf_op jit(solution)/shard_map/ppermute | solution.py:23
  11.9 0.3 fusion.37
  12.2 0.1 fusion.40
  12.2 0.5 fusion.30
  12.7 0.0 copy-start.1
  12.7 4.0 %multiply_subtract_fusion = (f32[64,40,384]{2,1,0:T(8,128)}, f32[64,40,384]{2,1,0:T(8,128)}) fusion(f32[40,384]{1,0:T(8,128)S(1)} %get-tuple-element.13, f32[64,384]{1,0:T(8,128)S(1)} %get-tuple-element.12, f32[40,384]{1,0:T(8,128)S(1)} %get-tuple-element.14, f32[64,384]{1,0:T(8,128)S(1)} %get-tuple-element.11), kind=kLoop, calls=%fused_computation.11 | loop fusion | flops 6881280 | bytes 8183808 | tf_op jit(solution)/shard_map/sub | solution.py:111
  16.7 0.2 convert_multiply_fusion
  16.9 0.7 copy-done.2
  17.6 0.0 copy-done.3
  17.7 0.7 pad.12.row_ref
  18.4 0.7 pad.13.col_ref
  19.1 0.0 collective-permute-done
  19.1 0.0 collective-permute-done.1
  19.1 1.1 maximum_bitcast_fusion.4
  20.1 0.9 pad.11.padded_ref
  21.1 10.6 %shard_map.82 = f32[2,2,8,2560]{3,2,1,0:T(8,128)} custom-call(f32[2,2,16,2560]{3,2,1,0:T(8,128)} %pad.11.padded_ref, s32[2,8,2560]{2,1,0:T(8,128)} %pad.12.row_ref, s32[2,8,2560]{2,1,0:T(8,128)} %pad.13.col_ref), custom_call_target="tpu_custom_call" | custom-call | tf_op jit(solution)/shard_map/pallas_call | solution.py:79
  31.7 8.1 %fusion.17 = f32[384,2,2,2,5]{0,4,1,3,2:T(8,128)S(1)} fusion(f32[1,2560,384]{2,1,0:T(8,128)} %bitcast.96, f32[1,2560,384]{2,1,0:T(8,128)} %bitcast.94, f32[2,2,8,2560]{3,2,1,0:T(8,128)} %shard_map.82), kind=kOutput, calls=%fused_computation.21 | convolution fusion | flops 475791360 | bytes 8253440 | tf_op jit(solution)/shard_map/lfpj,rjm->mfrlp/dot_general | solution.py:145
  39.8 0.0 copy-start.6
  39.8 5.2 %reshape.361 = f32[64,2,3,2,2,2,5]{2,1,0,5,6,4,3:T(2,128)} reshape(f32[384,2,2,2,5]{0,3,4,2,1:T(2,128)S(1)} %copy.56) | data formatting | bytes 122880 | tf_op jit(solution)/shard_map/reshape | solution.py:146
  45.1 3.1 %copy.57 = f32[64,2,2,2,3,2,5]{0,3,2,1,6,5,4:T(2,128)S(1)} copy(f32[64,2,2,2,3,2,5]{4,1,0,5,6,3,2:T(2,128)} %bitcast.98) | data formatting | bytes 122880 | tf_op jit(solution)/shard_map/transpose | solution.py:147
  48.1 0.1 copy.91
  48.2 0.8 reshape.377
  49.0 3.5 %all-to-all-start = ((f32[8,1,1920]{2,1,0:T(1,128)}), f32[8,1,1920]{2,1,0:T(1,128)S(1)}, u32[]{:S(2)}, u32[]{:S(2)}) async-start(f32[8,1,1920]{2,1,0:T(1,128)} %reshape.377), calls=%async_computation | async-start | bytes 122880 | tf_op jit(solution)/shard_map/all_to_all | solution.py:149
  52.5 4.1 %all-to-all-done = f32[8,1,1920]{2,1,0:T(1,128)S(1)} async-done(((f32[8,1,1920]{2,1,0:T(1,128)}), f32[8,1,1920]{2,1,0:T(1,128)S(1)}, u32[]{:S(2)}, u32[]{:S(2)}) %all-to-all-start) | async-done | bytes 61472 | tf_op jit(solution)/shard_map/all_to_all | solution.py:149
  56.6 0.6 broadcast.247
  57.2 0.8 reduce
  57.9 0.1 reshape.378
  58.1 1.7 %copy.59 = f32[64,1,3,2,4,2,5]{6,4,5,3,2,1,0:T(4,128)} copy(f32[64,1,3,2,4,2,5]{0,5,6,2,4,3,1:T(2,128)S(1)} %bitcast.106) | data formatting | bytes 122880 | tf_op jit(solution)/shard_map/reshape | solution.py:150
  59.7 3.8 %reshape.379 = f32[64,1,240]{2,1,0:T(1,128)} reshape(f32[64,1,3,2,2,4,5]{6,5,4,3,2,1,0:T(4,128)} %bitcast.99) | data formatting | bytes 122880
  63.5 18.3 %all-to-all-start.1 = ((f32[64,1,240]{2,1,0:T(1,128)}), f32[64,1,240]{2,1,0:T(1,128)S(1)}, u32[]{:S(2)}, u32[]{:S(2)}) async-start(f32[64,1,240]{2,1,0:T(1,128)} %reshape.379), calls=%async_computation.1 | async-start | bytes 131072 | tf_op jit(solution)/shard_map/all_to_all | solution.py:151
  81.8 0.0 copy-done.4
  81.9 0.2 mul.376
  82.1 0.1 copy.61
  82.2 2.7 %reshape.360 = f32[3,64,2,5,384]{4,3,2,1,0:T(8,128)} reshape(f32[3,640,384]{2,1,0:T(8,128)S(1)} %convert_multiply_fusion) | data formatting | bytes 5898240 | tf_op jit(solution)/shard_map/reshape | solution.py:155
  84.9 0.1 add_divide_fusion
  85.0 10.4 %all-to-all-done.1 = f32[64,1,240]{2,1,0:T(1,128)S(1)} async-done(((f32[64,1,240]{2,1,0:T(1,128)}), f32[64,1,240]{2,1,0:T(1,128)S(1)}, u32[]{:S(2)}, u32[]{:S(2)}) %all-to-all-start.1) | async-done | bytes 61472 | tf_op jit(solution)/shard_map/all_to_all | solution.py:151
  95.4 0.8 reduce.1
  96.1 1.8 %reshape.380 = f32[64,1,3,2,2,4,5]{6,5,4,3,2,1,0:T(4,128)S(1)} reshape(f32[64,240]{1,0:T(8,128)S(1)} %reduce.1) | data formatting | bytes 122880
  98.0 0.8 copy.60
  98.7 4.7 %fusion.20 = f32[8,3,384]{2,0,1:T(8,128)S(1)} fusion(f32[3,64,2,5,384]{4,3,2,1,0:T(8,128)} %reshape.360, f32[64,3,2,8,5]{0,3,4,2,1:T(8,128)S(1)} %bitcast.104, f32[64,2,5]{0,2,1:T(8,128)S(1)} %copy.61), kind=kOutput, calls=%fused_computation.22 | convolution fusion | flops 70794240 | bytes 3049984 | tf_op jit(solution)/shard_map/awblp,wabpn->lwn/dot_general | solution.py:157
  103.5 0.2 fusion.23
  103.7 0.2 convolution_bitcast_fusion
  103.9 7.4 %fusion.14 = f32[64,3,2,8,5]{0,3,4,2,1:T(8,128)S(1)} fusion(f32[8,3,384,1,1]{2,0,4,3,1:T(8,128)S(1)} %convolution_bitcast_fusion, f32[3,64,2,5,384]{4,3,2,1,0:T(8,128)} %reshape.360), kind=kOutput, calls=%fused_computation.20 | convolution fusion | flops 70778880 | bytes 3047424 | tf_op jit(solution)/shard_map/lwn,wabpn->awblp/dot_general | solution.py:161
  111.3 1.0 copy.65
  112.4 1.6 reshape.381
  113.9 5.3 %all-to-all-start.2 = ((f32[64,1,240]{2,1,0:T(1,128)}), f32[64,1,240]{2,1,0:T(1,128)S(1)}, u32[]{:S(2)}, u32[]{:S(2)}) async-start(f32[64,1,240]{2,1,0:T(1,128)} %reshape.381), calls=%async_computation.2 | async-start | bytes 131072 | tf_op jit(solution)/shard_map/all_to_all | solution.py:163
  119.2 13.5 %all-to-all-done.2 = f32[64,1,240]{2,1,0:T(1,128)S(1)} async-done(((f32[64,1,240]{2,1,0:T(1,128)}), f32[64,1,240]{2,1,0:T(1,128)S(1)}, u32[]{:S(2)}, u32[]{:S(2)}) %all-to-all-start.2) | async-done | bytes 61472 | tf_op jit(solution)/shard_map/all_to_all | solution.py:163
  132.7 0.8 reduce.2
  133.5 0.7 reshape.382
  134.2 0.3 bitcast_bitcast_fusion
  134.5 0.9 copy.66
  135.4 0.8 reshape.383
  136.2 5.9 %all-to-all-start.3 = ((f32[8,1,1920]{2,1,0:T(1,128)}), f32[8,1,1920]{2,1,0:T(1,128)S(1)}, u32[]{:S(2)}, u32[]{:S(2)}) async-start(f32[8,1,1920]{2,1,0:T(1,128)} %reshape.383), calls=%async_computation.3 | async-start | bytes 122880 | tf_op jit(solution)/shard_map/all_to_all | solution.py:164
  142.0 7.0 %broadcast_multiply_fusion.1 = (f32[1,2560,384]{2,1,0:T(8,128)}, f32[1,2560,384]{2,1,0:T(8,128)}) fusion(f32[384]{0:T(512)S(1)} %fusion.44, f32[1,2560,384]{2,1,0:T(8,128)} %bitcast.95, f32[1,2560,384]{2,1,0:T(8,128)} %bitcast.97), kind=kLoop, calls=%fused_computation.15 | loop fusion | flops 1966080 | bytes 15730176 | tf_op jit(solution)/shard_map/mul | solution.py:115
  149.0 0.0 all-to-all-done.3
  149.0 0.8 reduce.3
  149.8 0.1 reshape.384
  149.9 1.5 copy.76
  151.4 3.2 %reshape.376 = f32[2,2,2,5,384]{4,3,1,2,0:T(8,128)S(1)} reshape(f32[2,2,2,5,64,2,3]{6,5,4,3,1,2,0:T(2,128)S(1)} %copy.76) | data formatting | bytes 122880 | tf_op jit(solution)/shard_map/reshape | solution.py:166
  154.6 9.4 %fusion.9 = f32[2,5,2,2560]{3,1,2,0:T(8,128)S(1)} fusion(f32[2,2,2,5,384]{4,3,1,2,0:T(8,128)S(1)} %reshape.376, f32[1,2560,384]{2,1,0:T(8,128)} %get-tuple-element.10, f32[1,2560,384]{2,1,0:T(8,128)} %get-tuple-element.9), kind=kOutput, calls=%fused_computation.12 | convolution fusion | flops 473825280 | bytes 8130560 | tf_op jit(solution)/shard_map/frlpm,rjm->fplj/dot_general | solution.py:167
  164.1 0.8 copy.70
  (19 shorter events, 0.2 us)
Async XLA Ops:
  0.0 103.5 %copy-start = (f32[8,8]{1,0:T(8,128)S(1)}, f32[8,8]{1,0:T(8,128)}, u32[]{:S(2)}) copy-start(f32[8,8]{1,0:T(8,128)} %param.13) | copy-start | bytes 772
  1.8 17.3 %collective-permute-start = (f32[2,4,2,2560]{3,1,0,2:T(4,128)}, f32[2,4,2,2560]{3,1,0,2:T(4,128)S(1)}, u32[]{:S(2)}, u32[]{:S(2)}) collective-permute-start(f32[2,4,2,2560]{3,1,0,2:T(4,128)} %get-tuple-element.5), channel_id=1, source_target_pairs={{0,4},{4,8},{8,12},{12,16},{16,20},{20,24},{24,28},{28,32},{32,36}... | collective-permute-start | bytes 491528 | tf_op jit(solution)/shard_map/ppermute | solution.py:22
  6.7 12.4 %collective-permute-start.1 = (f32[2,4,2,2560]{3,1,0,2:T(4,128)}, f32[2,4,2,2560]{3,1,0,2:T(4,128)}, u32[]{:S(2)}, u32[]{:S(2)}) collective-permute-start(f32[2,4,2,2560]{3,1,0,2:T(4,128)} %get-tuple-element.6), channel_id=1, source_target_pairs={{4,0},{8,4},{12,8},{16,12},{20,16},{24,20},{28,24},{32,28},{36,32}... | collective-permute-start | bytes 491528 | tf_op jit(solution)/shard_map/ppermute | solution.py:23
  12.7 4.0 %copy-start.1 = (bf16[3,640,384]{2,1,0:T(8,128)(2,1)S(1)}, bf16[3,640,384]{2,1,0:T(8,128)(2,1)}, u32[]{:S(2)}) copy-start(bf16[3,640,384]{2,1,0:T(8,128)(2,1)} %param.11) | copy-start | bytes 4423684
  16.7 0.9 copy-start.2
  16.7 0.9 copy-start.3
  39.8 12.7 %copy-start.6 = (f32[8]{0:T(128)S(1)}, f32[8]{0:T(128)}, u32[]{:S(2)}) copy-start(f32[8]{0:T(128)} %param.15) | copy-start | bytes 100
  45.1 36.8 %copy-start.4 = (f32[640]{0:T(1024)S(1)}, f32[640]{0:T(1024)}, u32[]{:S(2)}) copy-start(f32[640]{0:T(1024)} %param.12) | copy-start | bytes 7684
  49.0 7.6 %all-to-all-start = ((f32[8,1,1920]{2,1,0:T(1,128)}), f32[8,1,1920]{2,1,0:T(1,128)S(1)}, u32[]{:S(2)}, u32[]{:S(2)}) async-start(f32[8,1,1920]{2,1,0:T(1,128)} %reshape.377), calls=%async_computation | async-start | bytes 122880 | tf_op jit(solution)/shard_map/all_to_all | solution.py:149
  63.5 31.9 %all-to-all-start.1 = ((f32[64,1,240]{2,1,0:T(1,128)}), f32[64,1,240]{2,1,0:T(1,128)S(1)}, u32[]{:S(2)}, u32[]{:S(2)}) async-start(f32[64,1,240]{2,1,0:T(1,128)} %reshape.379), calls=%async_computation.1 | async-start | bytes 131072 | tf_op jit(solution)/shard_map/all_to_all | solution.py:151
  84.9 18.8 %copy-start.5 = (f32[8,8]{1,0:T(8,128)S(1)}, f32[8,8]{1,0:T(8,128)}, u32[]{:S(2)}) copy-start(f32[8,8]{1,0:T(8,128)} %param.14) | copy-start | bytes 772
  113.9 18.8 %all-to-all-start.2 = ((f32[64,1,240]{2,1,0:T(1,128)}), f32[64,1,240]{2,1,0:T(1,128)S(1)}, u32[]{:S(2)}, u32[]{:S(2)}) async-start(f32[64,1,240]{2,1,0:T(1,128)} %reshape.381), calls=%async_computation.2 | async-start | bytes 131072 | tf_op jit(solution)/shard_map/all_to_all | solution.py:163
  136.2 12.8 %all-to-all-start.3 = ((f32[8,1,1920]{2,1,0:T(1,128)}), f32[8,1,1920]{2,1,0:T(1,128)S(1)}, u32[]{:S(2)}, u32[]{:S(2)}) async-start(f32[8,1,1920]{2,1,0:T(1,128)} %reshape.383), calls=%async_computation.3 | async-start | bytes 122880 | tf_op jit(solution)/shard_map/all_to_all | solution.py:164
where the time goes:
time: 166 us; the launch traced here: 165 us
  starting transfers between devices  43 us (26%)
  local copies, waits for them, and re-layouts  36.8 us (22%)
  matrix products  30 us (18%)
  waiting for transfers between devices  27.9 us (17%)
  other arithmetic  16.2 us (10%)
  Pallas kernels  10.6 us (6%)
    all_to_all x2, waiting for transfers between devices, per_device(): lax.all_to_all(staged, 'lo', split_axis=0, concat_axis=1, tiled=True)  23.9 us
    all_to_all x2, starting transfers between devices, per_device(): lax.all_to_all(staged, 'lo', split_axis=0, concat_axis=1, tiled=True)  23.6 us
    unnamed x25, local copies, waits for them, and re-layouts  11.4 us
    pallas_call x1, Pallas kernels, advect_kernel_call(): pl.pallas_call(advect_kernel, grid=(nlev,), in_specs=[pl.BlockSpec((1, nf...  10.6 us
    dot_general x1, matrix products, per_device(): return jnp.einsum('frlpm,rjm->fplj', by_lat, backward, precision=highest)  9.41 us
    dot_general x1, matrix products, per_device(): coeffs = jnp.einsum('lfpj,rjm->mfrlp', advected, forward, precision=highest)  8.05 us
    dot_general x1, matrix products, per_device(): gridded = jnp.einsum('lwn,wabpn->awblp', solved, basis, precision=highest)  7.44 us
    mul x1, other arithmetic, fourier_tables(): backward = jnp.stack([cosine * doubling, -sine_part * doubling], 0)  6.98 us
  transfers between devices with their start and end apart: 6, of which 3 were waited for; matrix products, arithmetic and copies ran while one was open for 10% of the time, Pallas kernels for 0%

commit v1 on v0

--- a/solution.py
+++ b/solution.py
@@ -12,6 +12,7 @@
 stencil_weights = (-0.0625, 0.5625, 0.5625, -0.0625)
 stiffness = 4.0
 highest = lax.Precision.HIGHEST
+three_pass = lax.Precision.HIGH
 
 LAT = ("lo", "lc")
 
@@ -142,7 +143,7 @@
         forward, backward = fourier_tables(nlon, cut_off)
         nr = forward.shape[0]
         split = (n_lo, n_lc, wave_dev)
-        coeffs = jnp.einsum("lfpj,rjm->mfrlp", advected, forward, precision=highest)
+        coeffs = jnp.einsum("lfpj,rjm->mfrlp", advected, forward, precision=three_pass)
         coeffs = coeffs.reshape(*split, nfield, nr, lev_dev, npoint)
         coeffs = jnp.transpose(coeffs, (0, 1, 3, 4, 2, 5, 6))
         coeffs = coeffs.reshape(n_lo, n_lc * nfield * nr, wave_dev, 1, lev_dev, npoint)
@@ -154,17 +155,17 @@
         basis = legendre.astype(jnp.float32) * triangle_mask(wave_first, wave_dev, cut_off)[:, None, :]
         basis = basis.reshape(wave_dev, n_lo, n_lc, npoint, cut_off)
         weights = lat_weights.reshape(n_lo, 1, n_lc, 1, npoint)
-        spectrum = jnp.einsum("awblp,wabpn->lwn", by_wave * weights, basis, precision=highest)
+        spectrum = jnp.einsum("awblp,wabpn->lwn", by_wave * weights, basis, precision=three_pass)
         modal = jnp.einsum("kl,lmn->kmn", to_modes, spectrum, precision=highest)
         scaled = modal * damping(mode_rates, cut_off, cut_off)[:, None, :]
         solved = jnp.einsum("lk,kmn->lmn", from_modes, scaled, precision=highest)
-        gridded = jnp.einsum("lwn,wabpn->awblp", solved, basis, precision=highest)
+        gridded = jnp.einsum("lwn,wabpn->awblp", solved, basis, precision=three_pass)
         staged = gridded.reshape(n_lo, 1, wave_dev, n_lc * n_lev, 1, lev_dev, npoint)
         staged = lax.all_to_all(staged, "lo", split_axis=0, concat_axis=1, tiled=True)
         staged = lax.all_to_all(staged, ("lc", "lev"), split_axis=3, concat_axis=4, tiled=True)
         by_lat = staged.reshape(n_lo, wave_dev, n_lc, nfield, nr, lev_dev, npoint)
         by_lat = jnp.transpose(by_lat, (3, 4, 5, 6, 0, 2, 1)).reshape(nfield, nr, lev_dev, npoint, cut_off)
-        return jnp.einsum("frlpm,rjm->fplj", by_lat, backward, precision=highest)
+        return jnp.einsum("frlpm,rjm->fplj", by_lat, backward, precision=three_pass)
 
     return per_device
 

time: 166 us -> 157 us (0.946)
  matrix products: 30 us -> 21.4 us
    dot_general x4, matrix products: 29.6 us -> 21.1 us  [the longest x1 6.82 us: per_device(): return jnp.einsum('frlpm,rjm->fplj', by_lat, backward, precision=three_pass)]
  transfers between devices with their start and end apart: 6 -> 6, of which waited for: 3 -> 3; matrix products, arithmetic and copies ran while one was open for 10% -> 11% of each run, Pallas kernels for 0% -> 0%
where the time goes in v1:
time: 157 us; the launch traced here: 156 us
  starting transfers between devices  43.2 us (28%)
  local copies, waits for them, and re-layouts  36.8 us (23%)
  waiting for transfers between devices  27.8 us (18%)
  matrix products  21.4 us (14%)
  other arithmetic  16.2 us (10%)
  Pallas kernels  10.6 us (7%)
    all_to_all x2, starting transfers between devices, per_device(): lax.all_to_all(staged, 'lo', split_axis=0, concat_axis=1, tiled=True)  23.8 us
    all_to_all x2, waiting for transfers between devices, per_device(): lax.all_to_all(staged, 'lo', split_axis=0, concat_axis=1, tiled=True)  23.7 us
    unnamed x25, local copies, waits for them, and re-layouts  11.4 us
    pallas_call x1, Pallas kernels, advect_kernel_call(): pl.pallas_call(advect_kernel, grid=(nlev,), in_specs=[pl.BlockSpec((1, nf...  10.6 us
    mul x1, other arithmetic, fourier_tables(): backward = jnp.stack([cosine * doubling, -sine_part * doubling], 0)  6.98 us
    dot_general x1, matrix products, per_device(): return jnp.einsum('frlpm,rjm->fplj', by_lat, backward, precision=three_pass)  6.82 us
    all_to_all x1, starting transfers between devices, per_device(): lax.all_to_all(staged, ('lc', 'lev'), split_axis=3, concat_axis=4, tiled=...  5.86 us
    dot_general x1, matrix products, per_device(): jnp.einsum('lfpj,rjm->mfrlp', advected, forward, precision=three_pass)  5.46 us
  transfers between devices with their start and end apart: 6, of which 3 were waited for; matrix products, arithmetic and copies ran while one was open for 11% of the time, Pallas kernels for 0%

profile of v1, /device:TPU:1, one launch (start us, length us, event | category | flops | bytes accessed | tf_op | source)
XLA Modules:
  0.0 156.3 jit_solution(16772266399479460431)
XLA Ops:
  0.0 0.0 copy-start
  0.0 1.0 copy.51
  1.0 0.8 fusion.48
  1.8 4.9 %collective-permute-start = (f32[2,4,2,2560]{3,1,0,2:T(4,128)}, f32[2,4,2,2560]{3,1,0,2:T(4,128)S(1)}, u32[]{:S(2)}, u32[]{:S(2)}) collective-permute-start(f32[2,4,2,2560]{3,1,0,2:T(4,128)} %get-tuple-element.5), channel_id=1, source_target_pairs={{0,4},{4,8},{8,12},{12,16},{16,20},{20,24},{24,28},{28,32},{32,36}... | collective-permute-start | bytes 491528 | tf_op jit(solution)/shard_map/ppermute | solution.py:23
  6.7 5.1 %collective-permute-start.1 = (f32[2,4,2,2560]{3,1,0,2:T(4,128)}, f32[2,4,2,2560]{3,1,0,2:T(4,128)}, u32[]{:S(2)}, u32[]{:S(2)}) collective-permute-start(f32[2,4,2,2560]{3,1,0,2:T(4,128)} %get-tuple-element.6), channel_id=1, source_target_pairs={{4,0},{8,4},{12,8},{16,12},{20,16},{24,20},{28,24},{32,28},{36,32}... | collective-permute-start | bytes 491528 | tf_op jit(solution)/shard_map/ppermute | solution.py:24
  11.9 0.3 fusion.37
  12.2 0.1 fusion.40
  12.2 0.5 fusion.30
  12.7 0.0 copy-start.1
  12.7 4.0 %multiply_subtract_fusion = (f32[64,40,384]{2,1,0:T(8,128)}, f32[64,40,384]{2,1,0:T(8,128)}) fusion(f32[40,384]{1,0:T(8,128)S(1)} %get-tuple-element.13, f32[64,384]{1,0:T(8,128)S(1)} %get-tuple-element.12, f32[40,384]{1,0:T(8,128)S(1)} %get-tuple-element.14, f32[64,384]{1,0:T(8,128)S(1)} %get-tuple-element.11), kind=kLoop, calls=%fused_computation.11 | loop fusion | flops 6881280 | bytes 8183808 | tf_op jit(solution)/shard_map/sub | solution.py:112
  16.7 0.2 convert_multiply_fusion
  16.9 0.7 copy-done.2
  17.6 0.0 copy-done.3
  17.7 0.7 pad.12.row_ref
  18.4 0.7 pad.13.col_ref
  19.1 0.0 collective-permute-done
  19.1 0.0 collective-permute-done.1
  19.1 1.1 maximum_bitcast_fusion.4
  20.1 0.9 pad.11.padded_ref
  21.1 10.6 %shard_map.82 = f32[2,2,8,2560]{3,2,1,0:T(8,128)} custom-call(f32[2,2,16,2560]{3,2,1,0:T(8,128)} %pad.11.padded_ref, s32[2,8,2560]{2,1,0:T(8,128)} %pad.12.row_ref, s32[2,8,2560]{2,1,0:T(8,128)} %pad.13.col_ref), custom_call_target="tpu_custom_call" | custom-call | tf_op jit(solution)/shard_map/pallas_call | solution.py:80
  31.7 5.5 %fusion.17 = f32[384,2,2,2,5]{0,4,1,3,2:T(8,128)S(1)} fusion(f32[1,2560,384]{2,1,0:T(8,128)} %bitcast.96, f32[1,2560,384]{2,1,0:T(8,128)} %bitcast.94, f32[2,2,8,2560]{3,2,1,0:T(8,128)} %shard_map.82), kind=kOutput, calls=%fused_computation.21 | convolution fusion | flops 239861760 | bytes 8253440 | tf_op jit(solution)/shard_map/lfpj,rjm->mfrlp/dot_general | solution.py:146
  37.2 0.0 copy-start.6
  37.3 5.2 %reshape.361 = f32[64,2,3,2,2,2,5]{2,1,0,5,6,4,3:T(2,128)} reshape(f32[384,2,2,2,5]{0,3,4,2,1:T(2,128)S(1)} %copy.56) | data formatting | bytes 122880 | tf_op jit(solution)/shard_map/reshape | solution.py:147
  42.5 3.1 %copy.57 = f32[64,2,2,2,3,2,5]{0,3,2,1,6,5,4:T(2,128)S(1)} copy(f32[64,2,2,2,3,2,5]{4,1,0,5,6,3,2:T(2,128)} %bitcast.98) | data formatting | bytes 122880 | tf_op jit(solution)/shard_map/transpose | solution.py:148
  45.6 0.1 copy.91
  45.6 0.8 reshape.377
  46.4 3.5 %all-to-all-start = ((f32[8,1,1920]{2,1,0:T(1,128)}), f32[8,1,1920]{2,1,0:T(1,128)S(1)}, u32[]{:S(2)}, u32[]{:S(2)}) async-start(f32[8,1,1920]{2,1,0:T(1,128)} %reshape.377), calls=%async_computation | async-start | bytes 122880 | tf_op jit(solution)/shard_map/all_to_all | solution.py:150
  49.9 4.1 %all-to-all-done = f32[8,1,1920]{2,1,0:T(1,128)S(1)} async-done(((f32[8,1,1920]{2,1,0:T(1,128)}), f32[8,1,1920]{2,1,0:T(1,128)S(1)}, u32[]{:S(2)}, u32[]{:S(2)}) %all-to-all-start) | async-done | bytes 61472 | tf_op jit(solution)/shard_map/all_to_all | solution.py:150
  54.0 0.6 broadcast.247
  54.6 0.8 reduce
  55.4 0.1 reshape.378
  55.5 1.7 %copy.59 = f32[64,1,3,2,4,2,5]{6,4,5,3,2,1,0:T(4,128)} copy(f32[64,1,3,2,4,2,5]{0,5,6,2,4,3,1:T(2,128)S(1)} %bitcast.106) | data formatting | bytes 122880 | tf_op jit(solution)/shard_map/reshape | solution.py:151
  57.2 3.8 %reshape.379 = f32[64,1,240]{2,1,0:T(1,128)} reshape(f32[64,1,3,2,2,4,5]{6,5,4,3,2,1,0:T(4,128)} %bitcast.99) | data formatting | bytes 122880
  60.9 18.3 %all-to-all-start.1 = ((f32[64,1,240]{2,1,0:T(1,128)}), f32[64,1,240]{2,1,0:T(1,128)S(1)}, u32[]{:S(2)}, u32[]{:S(2)}) async-start(f32[64,1,240]{2,1,0:T(1,128)} %reshape.379), calls=%async_computation.1 | async-start | bytes 131072 | tf_op jit(solution)/shard_map/all_to_all | solution.py:152
  79.3 0.2 mul.376
  79.5 0.1 copy.61
  79.6 2.7 %reshape.360 = f32[3,64,2,5,384]{4,3,2,1,0:T(8,128)} reshape(f32[3,640,384]{2,1,0:T(8,128)S(1)} %convert_multiply_fusion) | data formatting | bytes 5898240 | tf_op jit(solution)/shard_map/reshape | solution.py:156
  82.3 0.1 add_divide_fusion
  82.4 10.4 %all-to-all-done.1 = f32[64,1,240]{2,1,0:T(1,128)S(1)} async-done(((f32[64,1,240]{2,1,0:T(1,128)}), f32[64,1,240]{2,1,0:T(1,128)S(1)}, u32[]{:S(2)}, u32[]{:S(2)}) %all-to-all-start.1) | async-done | bytes 61472 | tf_op jit(solution)/shard_map/all_to_all | solution.py:152
  92.8 0.8 reduce.1
  93.5 1.8 %reshape.380 = f32[64,1,3,2,2,4,5]{6,5,4,3,2,1,0:T(4,128)S(1)} reshape(f32[64,240]{1,0:T(8,128)S(1)} %reduce.1) | data formatting | bytes 122880
  95.4 0.8 copy.60
  96.2 3.9 %fusion.20 = f32[8,3,384]{2,0,1:T(8,128)S(1)} fusion(f32[3,64,2,5,384]{4,3,2,1,0:T(8,128)} %reshape.360, f32[64,3,2,8,5]{0,3,4,2,1:T(8,128)S(1)} %bitcast.104, f32[64,2,5]{0,2,1:T(8,128)S(1)} %copy.61), kind=kOutput, calls=%fused_computation.22 | convolution fusion | flops 35404800 | bytes 3049984 | tf_op jit(solution)/shard_map/awblp,wabpn->lwn/dot_general | solution.py:158
  100.0 0.2 fusion.23
  100.2 0.2 convolution_bitcast_fusion
  100.4 4.9 %fusion.14 = f32[64,3,2,8,5]{0,3,4,2,1:T(8,128)S(1)} fusion(f32[8,3,384,1,1]{2,0,4,3,1:T(8,128)S(1)} %convolution_bitcast_fusion, f32[3,64,2,5,384]{4,3,2,1,0:T(8,128)} %reshape.360), kind=kOutput, calls=%fused_computation.20 | convolution fusion | flops 35389440 | bytes 3047424 | tf_op jit(solution)/shard_map/lwn,wabpn->awblp/dot_general | solution.py:162
  105.3 1.0 copy.65
  106.4 1.6 reshape.381
  107.9 5.5 %all-to-all-start.2 = ((f32[64,1,240]{2,1,0:T(1,128)}), f32[64,1,240]{2,1,0:T(1,128)S(1)}, u32[]{:S(2)}, u32[]{:S(2)}) async-start(f32[64,1,240]{2,1,0:T(1,128)} %reshape.381), calls=%async_computation.2 | async-start | bytes 131072 | tf_op jit(solution)/shard_map/all_to_all | solution.py:164
  113.4 13.3 %all-to-all-done.2 = f32[64,1,240]{2,1,0:T(1,128)S(1)} async-done(((f32[64,1,240]{2,1,0:T(1,128)}), f32[64,1,240]{2,1,0:T(1,128)S(1)}, u32[]{:S(2)}, u32[]{:S(2)}) %all-to-all-start.2) | async-done | bytes 61472 | tf_op jit(solution)/shard_map/all_to_all | solution.py:164
  126.7 0.8 reduce.2
  127.5 0.7 reshape.382
  128.2 0.3 bitcast_bitcast_fusion
  128.5 0.9 copy.66
  129.4 0.8 reshape.383
  130.2 5.9 %all-to-all-start.3 = ((f32[8,1,1920]{2,1,0:T(1,128)}), f32[8,1,1920]{2,1,0:T(1,128)S(1)}, u32[]{:S(2)}, u32[]{:S(2)}) async-start(f32[8,1,1920]{2,1,0:T(1,128)} %reshape.383), calls=%async_computation.3 | async-start | bytes 122880 | tf_op jit(solution)/shard_map/all_to_all | solution.py:165
  136.0 7.0 %broadcast_multiply_fusion.1 = (f32[1,2560,384]{2,1,0:T(8,128)}, f32[1,2560,384]{2,1,0:T(8,128)}) fusion(f32[384]{0:T(512)S(1)} %fusion.44, f32[1,2560,384]{2,1,0:T(8,128)} %bitcast.95, f32[1,2560,384]{2,1,0:T(8,128)} %bitcast.97), kind=kLoop, calls=%fused_computation.15 | loop fusion | flops 1966080 | bytes 15730176 | tf_op jit(solution)/shard_map/mul | solution.py:116
  143.0 0.0 all-to-all-done.3
  143.0 0.8 reduce.3
  143.8 0.1 reshape.384
  144.0 1.5 copy.76
  145.4 3.2 %reshape.376 = f32[2,2,2,5,384]{4,3,1,2,0:T(8,128)S(1)} reshape(f32[2,2,2,5,64,2,3]{6,5,4,3,1,2,0:T(2,128)S(1)} %copy.76) | data formatting | bytes 122880 | tf_op jit(solution)/shard_map/reshape | solution.py:167
  148.7 6.8 %fusion.9 = f32[2,5,2,2560]{3,1,2,0:T(8,128)S(1)} fusion(f32[2,2,2,5,384]{4,3,1,2,0:T(8,128)S(1)} %reshape.376, f32[1,2560,384]{2,1,0:T(8,128)} %get-tuple-element.10, f32[1,2560,384]{2,1,0:T(8,128)} %get-tuple-element.9), kind=kOutput, calls=%fused_computation.12 | convolution fusion | flops 237895680 | bytes 8130560 | tf_op jit(solution)/shard_map/frlpm,rjm->fplj/dot_general | solution.py:168
  155.5 0.8 copy.70
  (19 shorter events, 0.2 us)
Async XLA Ops:
  0.0 100.0 %copy-start = (f32[8,8]{1,0:T(8,128)S(1)}, f32[8,8]{1,0:T(8,128)}, u32[]{:S(2)}) copy-start(f32[8,8]{1,0:T(8,128)} %param.13) | copy-start | bytes 772
  1.8 17.3 %collective-permute-start = (f32[2,4,2,2560]{3,1,0,2:T(4,128)}, f32[2,4,2,2560]{3,1,0,2:T(4,128)S(1)}, u32[]{:S(2)}, u32[]{:S(2)}) collective-permute-start(f32[2,4,2,2560]{3,1,0,2:T(4,128)} %get-tuple-element.5), channel_id=1, source_target_pairs={{0,4},{4,8},{8,12},{12,16},{16,20},{20,24},{24,28},{28,32},{32,36}... | collective-permute-start | bytes 491528 | tf_op jit(solution)/shard_map/ppermute | solution.py:23
  6.7 12.4 %collective-permute-start.1 = (f32[2,4,2,2560]{3,1,0,2:T(4,128)}, f32[2,4,2,2560]{3,1,0,2:T(4,128)}, u32[]{:S(2)}, u32[]{:S(2)}) collective-permute-start(f32[2,4,2,2560]{3,1,0,2:T(4,128)} %get-tuple-element.6), channel_id=1, source_target_pairs={{4,0},{8,4},{12,8},{16,12},{20,16},{24,20},{28,24},{32,28},{36,32}... | collective-permute-start | bytes 491528 | tf_op jit(solution)/shard_map/ppermute | solution.py:24
  12.7 4.0 %copy-start.1 = (bf16[3,640,384]{2,1,0:T(8,128)(2,1)S(1)}, bf16[3,640,384]{2,1,0:T(8,128)(2,1)}, u32[]{:S(2)}) copy-start(bf16[3,640,384]{2,1,0:T(8,128)(2,1)} %param.11) | copy-start | bytes 4423684
  16.7 0.9 copy-start.2
  16.7 0.9 copy-start.3
  37.2 12.7 %copy-start.6 = (f32[8]{0:T(128)S(1)}, f32[8]{0:T(128)}, u32[]{:S(2)}) copy-start(f32[8]{0:T(128)} %param.15) | copy-start | bytes 100
  42.5 36.8 %copy-start.4 = (f32[640]{0:T(1024)S(1)}, f32[640]{0:T(1024)}, u32[]{:S(2)}) copy-start(f32[640]{0:T(1024)} %param.12) | copy-start | bytes 7684
  46.4 7.6 %all-to-all-start = ((f32[8,1,1920]{2,1,0:T(1,128)}), f32[8,1,1920]{2,1,0:T(1,128)S(1)}, u32[]{:S(2)}, u32[]{:S(2)}) async-start(f32[8,1,1920]{2,1,0:T(1,128)} %reshape.377), calls=%async_computation | async-start | bytes 122880 | tf_op jit(solution)/shard_map/all_to_all | solution.py:150
  60.9 31.9 %all-to-all-start.1 = ((f32[64,1,240]{2,1,0:T(1,128)}), f32[64,1,240]{2,1,0:T(1,128)S(1)}, u32[]{:S(2)}, u32[]{:S(2)}) async-start(f32[64,1,240]{2,1,0:T(1,128)} %reshape.379), calls=%async_computation.1 | async-start | bytes 131072 | tf_op jit(solution)/shard_map/all_to_all | solution.py:152
  82.3 17.9 %copy-start.5 = (f32[8,8]{1,0:T(8,128)S(1)}, f32[8,8]{1,0:T(8,128)}, u32[]{:S(2)}) copy-start(f32[8,8]{1,0:T(8,128)} %param.14) | copy-start | bytes 772
  107.9 18.8 %all-to-all-start.2 = ((f32[64,1,240]{2,1,0:T(1,128)}), f32[64,1,240]{2,1,0:T(1,128)S(1)}, u32[]{:S(2)}, u32[]{:S(2)}) async-start(f32[64,1,240]{2,1,0:T(1,128)} %reshape.381), calls=%async_computation.2 | async-start | bytes 131072 | tf_op jit(solution)/shard_map/all_to_all | solution.py:164
  130.2 12.8 %all-to-all-start.3 = ((f32[8,1,1920]{2,1,0:T(1,128)}), f32[8,1,1920]{2,1,0:T(1,128)S(1)}, u32[]{:S(2)}, u32[]{:S(2)}) async-start(f32[8,1,1920]{2,1,0:T(1,128)} %reshape.383), calls=%async_computation.3 | async-start | bytes 122880 | tf_op jit(solution)/shard_map/all_to_all | solution.py:165

commit v2 on v1

--- a/solution.py
+++ b/solution.py
@@ -111,10 +111,9 @@
     cos_f, sin_f = jnp.cos(fine)[None, :, :], jnp.sin(fine)[None, :, :]
     cosine = (cos_c * cos_f - sin_c * sin_f).reshape(nlon, cut_off)
     sine_part = (sin_c * cos_f + cos_c * sin_f).reshape(nlon, cut_off)
-    forward = jnp.stack([cosine, -sine_part], 0) / jnp.float32(nlon)
+    table = jnp.stack([cosine, -sine_part], 0)
     doubling = jnp.where(wave == 0, jnp.float32(1.0), jnp.float32(2.0))
-    backward = jnp.stack([cosine * doubling, -sine_part * doubling], 0)
-    return (forward, backward)
+    return (table, doubling)
 
 
 def triangle_mask(wave_first, wave_count, cut_off):
@@ -140,10 +139,10 @@
             jnp.transpose(dep_col, (1, 0, 2)),
             4,
         )
-        forward, backward = fourier_tables(nlon, cut_off)
-        nr = forward.shape[0]
+        table, doubling = fourier_tables(nlon, cut_off)
+        nr = table.shape[0]
         split = (n_lo, n_lc, wave_dev)
-        coeffs = jnp.einsum("lfpj,rjm->mfrlp", advected, forward, precision=three_pass)
+        coeffs = jnp.einsum("lfpj,rjm->mfrlp", advected, table, precision=three_pass) / jnp.float32(nlon)
         coeffs = coeffs.reshape(*split, nfield, nr, lev_dev, npoint)
         coeffs = jnp.transpose(coeffs, (0, 1, 3, 4, 2, 5, 6))
         coeffs = coeffs.reshape(n_lo, n_lc * nfield * nr, wave_dev, 1, lev_dev, npoint)
@@ -165,7 +164,7 @@
         staged = lax.all_to_all(staged, ("lc", "lev"), split_axis=3, concat_axis=4, tiled=True)
         by_lat = staged.reshape(n_lo, wave_dev, n_lc, nfield, nr, lev_dev, npoint)
         by_lat = jnp.transpose(by_lat, (3, 4, 5, 6, 0, 2, 1)).reshape(nfield, nr, lev_dev, npoint, cut_off)
-        return jnp.einsum("frlpm,rjm->fplj", by_lat, backward, precision=three_pass)
+        return jnp.einsum("frlpm,rjm->fplj", by_lat * doubling, table, precision=three_pass)
 
     return per_device
 

time: 157 us -> 154 us (0.981)
  blocking collectives: 0 us -> 18.6 us
  waiting for transfers between devices: 27.8 us -> 19.5 us
  other arithmetic: 16.2 us -> 9.34 us
  starting transfers between devices: 43.2 us -> 37.7 us
    all_to_all x0 -> x1, blocking collectives: none -> 18.6 us  [per_device(): lax.all_to_all(staged, 'lo', split_axis=0, concat_axis=1, tiled=True)]
    all_to_all x2 -> x1, waiting for transfers between devices: 23.7 us -> 10.5 us  [per_device(): lax.all_to_all(staged, 'lo', split_axis=0, concat_axis=1, tiled=True)]
    mul x1, other arithmetic: 6.98 us -> 0.02 us  [per_device(): by_lat * doubling]
    all_to_all x2 -> x1, starting transfers between devices: 23.8 us -> 18.3 us  [per_device(): lax.all_to_all(staged, 'lo', split_axis=0, concat_axis=1, tiled=True)]
    all_to_all x1, waiting for transfers between devices: 0.01 us -> 4.95 us  [per_device(): lax.all_to_all(staged, ('lc', 'lev'), split_axis=3, concat_axis=4, tiled=...]
    reshape x2 -> x1, local copies, waits for them, and re-layouts: 4.71 us -> 3.42 us  [per_device(): jnp.transpose(by_lat, (3, 4, 5, 6, 0, 2, 1))]
  transfers between devices with their start and end apart: 6 -> 5, of which waited for: 3 -> 3; matrix products, arithmetic and copies ran while one was open for 11% -> 6% of each run, Pallas kernels for 0% -> 0%
where the time goes in v2:
time: 154 us; the launch traced here: 153 us
  starting transfers between devices  37.7 us (24%)
  local copies, waits for them, and re-layouts  36 us (23%)
  matrix products  21.3 us (14%)
  waiting for transfers between devices  19.5 us (13%)
  blocking collectives  18.6 us (12%)
  Pallas kernels  10.6 us (7%)
  other arithmetic  9.34 us (6%)
    all_to_all x1, blocking collectives, per_device(): lax.all_to_all(staged, 'lo', split_axis=0, concat_axis=1, tiled=True)  18.6 us
    all_to_all x1, starting transfers between devices, per_device(): lax.all_to_all(staged, 'lo', split_axis=0, concat_axis=1, tiled=True)  18.3 us
    unnamed x25, local copies, waits for them, and re-layouts  10.8 us
    pallas_call x1, Pallas kernels, advect_kernel_call(): pl.pallas_call(advect_kernel, grid=(nlev,), in_specs=[pl.BlockSpec((1, nf...  10.6 us
    all_to_all x1, waiting for transfers between devices, per_device(): lax.all_to_all(staged, 'lo', split_axis=0, concat_axis=1, tiled=True)  10.5 us
    dot_general x1, matrix products, per_device(): jnp.einsum('frlpm,rjm->fplj', by_lat * doubling, table, precision=three_p...  6.81 us
    all_to_all x1, starting transfers between devices, per_device(): lax.all_to_all(staged, ('lc', 'lev'), split_axis=3, concat_axis=4, tiled=...  5.84 us
    dot_general x1, matrix products, per_device(): jnp.einsum('lfpj,rjm->mfrlp', advected, table, precision=three_pass)  5.4 us
  transfers between devices with their start and end apart: 5, of which 3 were waited for; matrix products, arithmetic and copies ran while one was open for 6% of the time, Pallas kernels for 0%

profile of v2, /device:TPU:1, one launch (start us, length us, event | category | flops | bytes accessed | tf_op | source)
XLA Modules:
  0.0 153.4 jit_solution(12349728433562007566)
XLA Ops:
  0.0 0.0 copy-start
  0.0 1.0 copy.51
  1.0 0.8 fusion.48
  1.8 4.9 %collective-permute-start = (f32[2,4,2,2560]{3,1,0,2:T(4,128)}, f32[2,4,2,2560]{3,1,0,2:T(4,128)S(1)}, u32[]{:S(2)}, u32[]{:S(2)}) collective-permute-start(f32[2,4,2,2560]{3,1,0,2:T(4,128)} %get-tuple-element.5), channel_id=1, source_target_pairs={{0,4},{4,8},{8,12},{12,16},{16,20},{20,24},{24,28},{28,32},{32,36}... | collective-permute-start | bytes 491528 | tf_op jit(solution)/shard_map/ppermute | solution.py:23
  6.7 5.1 %collective-permute-start.1 = (f32[2,4,2,2560]{3,1,0,2:T(4,128)}, f32[2,4,2,2560]{3,1,0,2:T(4,128)}, u32[]{:S(2)}, u32[]{:S(2)}) collective-permute-start(f32[2,4,2,2560]{3,1,0,2:T(4,128)} %get-tuple-element.6), channel_id=1, source_target_pairs={{4,0},{8,4},{12,8},{16,12},{20,16},{24,20},{28,24},{32,28},{36,32}... | collective-permute-start | bytes 491528 | tf_op jit(solution)/shard_map/ppermute | solution.py:24
  11.9 0.3 fusion.38
  12.2 0.1 fusion.41
  12.2 0.5 fusion.31
  12.7 0.0 copy-start.1
  12.7 4.0 %multiply_subtract_fusion = (f32[64,40,384]{2,1,0:T(8,128)}, f32[64,40,384]{2,1,0:T(8,128)}) fusion(f32[40,384]{1,0:T(8,128)S(1)} %get-tuple-element.11, f32[64,384]{1,0:T(8,128)S(1)} %get-tuple-element.10, f32[40,384]{1,0:T(8,128)S(1)} %get-tuple-element.12, f32[64,384]{1,0:T(8,128)S(1)} %get-tuple-element.9), kind=kLoop, calls=%fused_computation.6 | loop fusion | flops 6881280 | bytes 8183808 | tf_op jit(solution)/shard_map/sub | solution.py:112
  16.7 0.0 copy-done.1
  16.7 0.2 convert_multiply_fusion
  16.9 0.7 copy-done.2
  17.7 0.0 copy-done.3
  17.7 0.7 pad.12.row_ref
  18.4 0.7 pad.13.col_ref
  19.1 0.0 collective-permute-done
  19.1 0.0 collective-permute-done.1
  19.1 1.1 maximum_bitcast_fusion
  20.1 0.9 pad.11.padded_ref
  21.0 10.6 %shard_map.82 = f32[2,2,8,2560]{3,2,1,0:T(8,128)} custom-call(f32[2,2,16,2560]{3,2,1,0:T(8,128)} %pad.11.padded_ref, s32[2,8,2560]{2,1,0:T(8,128)} %pad.12.row_ref, s32[2,8,2560]{2,1,0:T(8,128)} %pad.13.col_ref), custom_call_target="tpu_custom_call" | custom-call | tf_op jit(solution)/shard_map/pallas_call | solution.py:80
  31.7 5.4 %fusion.17 = f32[384,2,2,2,5]{0,4,1,3,2:T(8,128)S(1)} fusion(f32[1,2560,384]{2,1,0:T(8,128)} %bitcast.93, f32[1,2560,384]{2,1,0:T(8,128)} %bitcast.91, f32[2,2,8,2560]{3,2,1,0:T(8,128)} %shard_map.82), kind=kOutput, calls=%fused_computation.15 | convolution fusion | flops 237911040 | bytes 8253440 | tf_op jit(solution)/shard_map/lfpj,rjm->mfrlp/dot_general | solution.py:145
  37.1 0.0 copy-start.6
  37.1 5.2 %reshape.277 = f32[64,2,3,2,2,2,5]{2,1,0,5,6,4,3:T(2,128)} reshape(f32[384,2,2,2,5]{0,3,4,2,1:T(2,128)S(1)} %copy.56) | data formatting | bytes 122880 | tf_op jit(solution)/shard_map/reshape | solution.py:146
  42.3 3.1 %copy.57 = f32[64,2,2,2,3,2,5]{0,3,2,1,6,5,4:T(2,128)S(1)} copy(f32[64,2,2,2,3,2,5]{4,1,0,5,6,3,2:T(2,128)} %bitcast.95) | data formatting | bytes 122880 | tf_op jit(solution)/shard_map/transpose | solution.py:147
  45.4 0.1 copy.91
  45.5 0.8 reshape.291
  46.2 3.5 %all-to-all-start = ((f32[8,1,1920]{2,1,0:T(1,128)}), f32[8,1,1920]{2,1,0:T(1,128)S(1)}, u32[]{:S(2)}, u32[]{:S(2)}) async-start(f32[8,1,1920]{2,1,0:T(1,128)} %reshape.291), calls=%async_computation | async-start | bytes 122880 | tf_op jit(solution)/shard_map/all_to_all | solution.py:149
  49.8 4.1 %all-to-all-done = f32[8,1,1920]{2,1,0:T(1,128)S(1)} async-done(((f32[8,1,1920]{2,1,0:T(1,128)}), f32[8,1,1920]{2,1,0:T(1,128)S(1)}, u32[]{:S(2)}, u32[]{:S(2)}) %all-to-all-start) | async-done | bytes 61472 | tf_op jit(solution)/shard_map/all_to_all | solution.py:149
  53.9 0.5 broadcast.204
  54.4 0.8 reduce
  55.2 0.1 reshape.292
  55.3 1.6 %copy.59 = f32[64,1,3,2,4,2,5]{6,4,5,3,2,1,0:T(4,128)} copy(f32[64,1,3,2,4,2,5]{0,5,6,2,4,3,1:T(2,128)S(1)} %bitcast.103) | data formatting | bytes 122880 | tf_op jit(solution)/shard_map/reshape | solution.py:150
  56.9 3.8 %reshape.293 = f32[64,1,240]{2,1,0:T(1,128)} reshape(f32[64,1,3,2,2,4,5]{6,5,4,3,2,1,0:T(4,128)} %bitcast.96) | data formatting | bytes 122880
  60.7 18.3 %all-to-all-start.1 = ((f32[64,1,240]{2,1,0:T(1,128)}), f32[64,1,240]{2,1,0:T(1,128)S(1)}, u32[]{:S(2)}, u32[]{:S(2)}) async-start(f32[64,1,240]{2,1,0:T(1,128)} %reshape.293), calls=%async_computation.1 | async-start | bytes 131072 | tf_op jit(solution)/shard_map/all_to_all | solution.py:151
  79.0 0.2 mul.273
  79.3 0.1 copy.61
  79.3 2.6 %reshape.276 = f32[3,64,2,5,384]{4,3,2,1,0:T(8,128)} reshape(f32[3,640,384]{2,1,0:T(8,128)S(1)} %convert_multiply_fusion) | data formatting | bytes 5898240 | tf_op jit(solution)/shard_map/reshape | solution.py:155
  82.0 0.1 add_divide_fusion
  82.0 10.5 %all-to-all-done.1 = f32[64,1,240]{2,1,0:T(1,128)S(1)} async-done(((f32[64,1,240]{2,1,0:T(1,128)}), f32[64,1,240]{2,1,0:T(1,128)S(1)}, u32[]{:S(2)}, u32[]{:S(2)}) %all-to-all-start.1) | async-done | bytes 61472 | tf_op jit(solution)/shard_map/all_to_all | solution.py:151
  92.5 0.8 reduce.1
  93.3 1.8 %reshape.294 = f32[64,1,3,2,2,4,5]{6,5,4,3,2,1,0:T(4,128)S(1)} reshape(f32[64,240]{1,0:T(8,128)S(1)} %reduce.1) | data formatting | bytes 122880
  95.2 0.8 copy.60
  95.9 3.9 %fusion.20 = f32[8,3,384]{2,0,1:T(8,128)S(1)} fusion(f32[3,64,2,5,384]{4,3,2,1,0:T(8,128)} %reshape.276, f32[64,3,2,8,5]{0,3,4,2,1:T(8,128)S(1)} %bitcast.101, f32[64,2,5]{0,2,1:T(8,128)S(1)} %copy.61), kind=kOutput, calls=%fused_computation.16 | convolution fusion | flops 35404800 | bytes 3049984 | tf_op jit(solution)/shard_map/awblp,wabpn->lwn/dot_general | solution.py:157
  99.8 0.0 copy-done
  99.8 0.2 fusion.23
  100.0 0.2 convolution_bitcast_fusion
  100.1 4.9 %fusion.11 = f32[64,3,2,8,5]{0,3,4,2,1:T(8,128)S(1)} fusion(f32[8,3,384,1,1]{2,0,4,3,1:T(8,128)S(1)} %convolution_bitcast_fusion, f32[3,64,2,5,384]{4,3,2,1,0:T(8,128)} %reshape.276), kind=kOutput, calls=%fused_computation.13 | convolution fusion | flops 35389440 | bytes 3047424 | tf_op jit(solution)/shard_map/lwn,wabpn->awblp/dot_general | solution.py:161
  105.1 1.0 copy.65
  106.1 0.9 reshape.295
  107.1 18.6 %all_to_all.45 = f32[64,1,240]{2,1,0:T(1,128)S(1)} all-to-all(f32[64,1,240]{2,1,0:T(1,128)S(1)} %reshape.295), channel_id=1, replica_groups=mesh['lo'=64,'lc'=2,'lev'=4] {'lo'}, dimensions={0} | all-to-all | bytes 122880 | tf_op jit(solution)/shard_map/all_to_all | solution.py:163
  125.6 0.8 reduce.2
  126.4 0.7 reshape.296
  127.1 0.3 bitcast_bitcast_fusion
  127.5 0.9 copy.66
  128.4 0.8 reshape.297
  129.1 5.8 %all-to-all-start.3 = ((f32[8,1,1920]{2,1,0:T(1,128)}), f32[8,1,1920]{2,1,0:T(1,128)S(1)}, u32[]{:S(2)}, u32[]{:S(2)}) async-start(f32[8,1,1920]{2,1,0:T(1,128)} %reshape.297), calls=%async_computation.3 | async-start | bytes 122880 | tf_op jit(solution)/shard_map/all_to_all | solution.py:164
  135.0 4.9 %all-to-all-done.3 = f32[8,1,1920]{2,1,0:T(1,128)S(1)} async-done(((f32[8,1,1920]{2,1,0:T(1,128)}), f32[8,1,1920]{2,1,0:T(1,128)S(1)}, u32[]{:S(2)}, u32[]{:S(2)}) %all-to-all-start.3) | async-done | bytes 61472 | tf_op jit(solution)/shard_map/all_to_all | solution.py:164
  139.9 0.8 reduce.3
  140.7 0.1 reshape.298
  140.9 1.5 copy.68
  142.3 3.4 %reshape.283 = f32[2,2,2,5,384]{4,2,3,1,0:T(2,128)S(1)} reshape(f32[2,2,2,5,64,2,3]{6,5,4,2,3,1,0:T(2,128)S(1)} %copy.68) | data formatting | bytes 122880 | tf_op jit(solution)/shard_map/reshape | solution.py:166
  145.8 6.8 %fusion.4 = f32[2,5,2,2560]{3,1,2,0:T(8,128)S(1)} fusion(f32[1,2560,384]{2,1,0:T(8,128)} %bitcast.94, f32[1,2560,384]{2,1,0:T(8,128)} %bitcast.92, f32[2,2,2,5,384]{4,2,3,1,0:T(2,128)S(1)} %broadcast_multiply_fusion), kind=kOutput, calls=%fused_computation.7 | convolution fusion | flops 237895680 | bytes 8130560 | tf_op jit(solution)/shard_map/frlpm,rjm->fplj/dot_general | solution.py:167
  152.6 0.8 copy.70
  (18 shorter events, 0.2 us)
Async XLA Ops:
  0.0 99.8 %copy-start = (f32[8,8]{1,0:T(8,128)S(1)}, f32[8,8]{1,0:T(8,128)}, u32[]{:S(2)}) copy-start(f32[8,8]{1,0:T(8,128)} %param.13) | copy-start | bytes 772
  1.8 17.3 %collective-permute-start = (f32[2,4,2,2560]{3,1,0,2:T(4,128)}, f32[2,4,2,2560]{3,1,0,2:T(4,128)S(1)}, u32[]{:S(2)}, u32[]{:S(2)}) collective-permute-start(f32[2,4,2,2560]{3,1,0,2:T(4,128)} %get-tuple-element.5), channel_id=1, source_target_pairs={{0,4},{4,8},{8,12},{12,16},{16,20},{20,24},{24,28},{28,32},{32,36}... | collective-permute-start | bytes 491528 | tf_op jit(solution)/shard_map/ppermute | solution.py:23
  6.7 12.4 %collective-permute-start.1 = (f32[2,4,2,2560]{3,1,0,2:T(4,128)}, f32[2,4,2,2560]{3,1,0,2:T(4,128)}, u32[]{:S(2)}, u32[]{:S(2)}) collective-permute-start(f32[2,4,2,2560]{3,1,0,2:T(4,128)} %get-tuple-element.6), channel_id=1, source_target_pairs={{4,0},{8,4},{12,8},{16,12},{20,16},{24,20},{28,24},{32,28},{36,32}... | collective-permute-start | bytes 491528 | tf_op jit(solution)/shard_map/ppermute | solution.py:24
  12.7 4.0 %copy-start.1 = (bf16[3,640,384]{2,1,0:T(8,128)(2,1)S(1)}, bf16[3,640,384]{2,1,0:T(8,128)(2,1)}, u32[]{:S(2)}) copy-start(bf16[3,640,384]{2,1,0:T(8,128)(2,1)} %param.11) | copy-start | bytes 4423684
  16.7 0.9 copy-start.2
  16.7 0.9 copy-start.3
  37.1 12.7 %copy-start.6 = (f32[8]{0:T(128)S(1)}, f32[8]{0:T(128)}, u32[]{:S(2)}) copy-start(f32[8]{0:T(128)} %param.15) | copy-start | bytes 100
  42.3 36.7 %copy-start.4 = (f32[640]{0:T(1024)S(1)}, f32[640]{0:T(1024)}, u32[]{:S(2)}) copy-start(f32[640]{0:T(1024)} %param.12) | copy-start | bytes 7684
  46.2 7.6 %all-to-all-start = ((f32[8,1,1920]{2,1,0:T(1,128)}), f32[8,1,1920]{2,1,0:T(1,128)S(1)}, u32[]{:S(2)}, u32[]{:S(2)}) async-start(f32[8,1,1920]{2,1,0:T(1,128)} %reshape.291), calls=%async_computation | async-start | bytes 122880 | tf_op jit(solution)/shard_map/all_to_all | solution.py:149
  60.7 31.9 %all-to-all-start.1 = ((f32[64,1,240]{2,1,0:T(1,128)}), f32[64,1,240]{2,1,0:T(1,128)S(1)}, u32[]{:S(2)}, u32[]{:S(2)}) async-start(f32[64,1,240]{2,1,0:T(1,128)} %reshape.293), calls=%async_computation.1 | async-start | bytes 131072 | tf_op jit(solution)/shard_map/all_to_all | solution.py:151
  82.0 18.0 %copy-start.5 = (f32[8,8]{1,0:T(8,128)S(1)}, f32[8,8]{1,0:T(8,128)}, u32[]{:S(2)}) copy-start(f32[8,8]{1,0:T(8,128)} %param.14) | copy-start | bytes 772
  129.1 10.8 %all-to-all-start.3 = ((f32[8,1,1920]{2,1,0:T(1,128)}), f32[8,1,1920]{2,1,0:T(1,128)S(1)}, u32[]{:S(2)}, u32[]{:S(2)}) async-start(f32[8,1,1920]{2,1,0:T(1,128)} %reshape.297), calls=%async_computation.3 | async-start | bytes 122880 | tf_op jit(solution)/shard_map/all_to_all | solution.py:164

commit v3 on v2

--- a/solution.py
+++ b/solution.py
@@ -48,7 +48,7 @@
     return result
 
 
-def advect_kernel(padded_ref, row_ref, col_ref, out_ref, weight_ref):
+def advect_kernel(padded_ref, row_ref, col_ref, out_ref, weight_ref, rolled_ref):
     nfield = padded_ref.shape[1]
     npoint, nlon = row_ref.shape[1], row_ref.shape[2]
     dep_col = col_ref[0]
@@ -56,14 +56,15 @@
         weight_ref[index] = tap_weight(dep_col, shift)
     dep_row = row_ref[0]
     for field in range(nfield):
+        block = padded_ref[0, field]
+        for index, shift in enumerate(range(-5, 7)):
+            rolled_ref[index] = pltpu.roll(block, (-shift) % nlon, 1) if shift % nlon else block
         result = None
         for row_shift in range(-3, 5):
             first = 4 + row_shift
-            rows = padded_ref[0, field, first : first + npoint, :]
             inner = None
-            for index, shift in enumerate(range(-5, 7)):
-                rolled = pltpu.roll(rows, (-shift) % nlon, 1) if shift % nlon else rows
-                term = weight_ref[index] * rolled
+            for index in range(12):
+                term = weight_ref[index] * rolled_ref[index, first : first + npoint, :]
                 inner = term if inner is None else inner + term
             term = tap_weight(dep_row, row_shift) * inner
             result = term if result is None else result + term
@@ -87,7 +88,7 @@
         ],
         out_specs=pl.BlockSpec((1, nfield, tall, nlon), lambda l: (l, 0, 0, 0)),
         out_shape=jax.ShapeDtypeStruct((nlev, nfield, tall, nlon), jnp.float32),
-        scratch_shapes=[pltpu.VMEM((12, tall, nlon), jnp.float32)],
+        scratch_shapes=[pltpu.VMEM((12, tall, nlon), jnp.float32), pltpu.VMEM((12, tall + 8, nlon), jnp.float32)],
         interpret=interpret,
     )(padded, dep_row, dep_col)
     return out[:, :, :npoint]

time: 154 us -> 152 us (0.987)
  Pallas kernels: 10.6 us -> 8.73 us
    pallas_call x1, Pallas kernels: 10.6 us -> 8.73 us  [advect_kernel_call(): pl.pallas_call(advect_kernel, grid=(nlev,), in_specs=[pl.BlockSpec((1, nf...]
where the time goes in v3:
time: 152 us
  starting transfers between devices  37.7 us (25%)
  local copies, waits for them, and re-layouts  36 us (24%)
  matrix products  21.3 us (14%)
  waiting for transfers between devices  19.5 us (13%)
  blocking collectives  18.6 us (12%)
  other arithmetic  9.34 us (6%)
  Pallas kernels  8.73 us (6%)
    all_to_all x1, blocking collectives, per_device(): lax.all_to_all(staged, 'lo', split_axis=0, concat_axis=1, tiled=True)  18.6 us
    all_to_all x1, starting transfers between devices, per_device(): lax.all_to_all(staged, 'lo', split_axis=0, concat_axis=1, tiled=True)  18.3 us
    unnamed x25, local copies, waits for them, and re-layouts  10.8 us
    all_to_all x1, waiting for transfers between devices, per_device(): lax.all_to_all(staged, 'lo', split_axis=0, concat_axis=1, tiled=True)  10.5 us
    pallas_call x1, Pallas kernels, advect_kernel_call(): pl.pallas_call(advect_kernel, grid=(nlev,), in_specs=[pl.BlockSpec((1, nf...  8.73 us
    dot_general x1, matrix products, per_device(): jnp.einsum('frlpm,rjm->fplj', by_lat * doubling, table, precision=three_p...  6.81 us
    all_to_all x1, starting transfers between devices, per_device(): lax.all_to_all(staged, ('lc', 'lev'), split_axis=3, concat_axis=4, tiled=...  5.84 us
    dot_general x1, matrix products, per_device(): jnp.einsum('lfpj,rjm->mfrlp', advected, table, precision=three_pass)  5.41 us
  transfers between devices with their start and end apart: 5, of which 3 were waited for; matrix products, arithmetic and copies ran while one was open for 6% of the time, Pallas kernels for 0%

profile of v3, /device:TPU:1, one launch (start us, length us, event | category | flops | bytes accessed | tf_op | source)
XLA Modules:
  0.0 151.5 jit_solution(14121847395018467727)
XLA Ops:
  0.0 0.0 copy-start
  0.0 1.0 copy.51
  1.0 0.8 fusion.48
  1.8 4.9 %collective-permute-start = (f32[2,4,2,2560]{3,1,0,2:T(4,128)}, f32[2,4,2,2560]{3,1,0,2:T(4,128)S(1)}, u32[]{:S(2)}, u32[]{:S(2)}) collective-permute-start(f32[2,4,2,2560]{3,1,0,2:T(4,128)} %get-tuple-element.5), channel_id=1, source_target_pairs={{0,4},{4,8},{8,12},{12,16},{16,20},{20,24},{24,28},{28,32},{32,36}... | collective-permute-start | bytes 491528 | tf_op jit(solution)/shard_map/ppermute | solution.py:23
  6.7 5.1 %collective-permute-start.1 = (f32[2,4,2,2560]{3,1,0,2:T(4,128)}, f32[2,4,2,2560]{3,1,0,2:T(4,128)}, u32[]{:S(2)}, u32[]{:S(2)}) collective-permute-start(f32[2,4,2,2560]{3,1,0,2:T(4,128)} %get-tuple-element.6), channel_id=1, source_target_pairs={{4,0},{8,4},{12,8},{16,12},{20,16},{24,20},{28,24},{32,28},{36,32}... | collective-permute-start | bytes 491528 | tf_op jit(solution)/shard_map/ppermute | solution.py:24
  11.9 0.3 fusion.38
  12.2 0.1 fusion.41
  12.2 0.5 fusion.31
  12.7 0.0 copy-start.1
  12.7 4.0 %multiply_subtract_fusion = (f32[64,40,384]{2,1,0:T(8,128)}, f32[64,40,384]{2,1,0:T(8,128)}) fusion(f32[40,384]{1,0:T(8,128)S(1)} %get-tuple-element.11, f32[64,384]{1,0:T(8,128)S(1)} %get-tuple-element.10, f32[40,384]{1,0:T(8,128)S(1)} %get-tuple-element.12, f32[64,384]{1,0:T(8,128)S(1)} %get-tuple-element.9), kind=kLoop, calls=%fused_computation.6 | loop fusion | flops 6881280 | bytes 8183808 | tf_op jit(solution)/shard_map/sub | solution.py:113
  16.7 0.0 copy-done.1
  16.7 0.2 convert_multiply_fusion
  16.9 0.7 copy-done.2
  17.7 0.0 copy-done.3
  17.7 0.7 pad.12.row_ref
  18.4 0.7 pad.13.col_ref
  19.1 0.0 collective-permute-done
  19.1 0.0 collective-permute-done.1
  19.1 1.1 maximum_bitcast_fusion
  20.1 0.9 pad.11.padded_ref
  21.0 8.7 %shard_map.82 = f32[2,2,8,2560]{3,2,1,0:T(8,128)} custom-call(f32[2,2,16,2560]{3,2,1,0:T(8,128)} %pad.11.padded_ref, s32[2,8,2560]{2,1,0:T(8,128)} %pad.12.row_ref, s32[2,8,2560]{2,1,0:T(8,128)} %pad.13.col_ref), custom_call_target="tpu_custom_call" | custom-call | tf_op jit(solution)/shard_map/pallas_call | solution.py:81
  29.8 5.4 %fusion.17 = f32[384,2,2,2,5]{0,4,1,3,2:T(8,128)S(1)} fusion(f32[1,2560,384]{2,1,0:T(8,128)} %bitcast.93, f32[1,2560,384]{2,1,0:T(8,128)} %bitcast.91, f32[2,2,8,2560]{3,2,1,0:T(8,128)} %shard_map.82), kind=kOutput, calls=%fused_computation.15 | convolution fusion | flops 237911040 | bytes 8253440 | tf_op jit(solution)/shard_map/lfpj,rjm->mfrlp/dot_general | solution.py:146
  35.2 0.0 copy-start.6
  35.2 5.2 %reshape.277 = f32[64,2,3,2,2,2,5]{2,1,0,5,6,4,3:T(2,128)} reshape(f32[384,2,2,2,5]{0,3,4,2,1:T(2,128)S(1)} %copy.56) | data formatting | bytes 122880 | tf_op jit(solution)/shard_map/reshape | solution.py:147
  40.4 3.1 %copy.57 = f32[64,2,2,2,3,2,5]{0,3,2,1,6,5,4:T(2,128)S(1)} copy(f32[64,2,2,2,3,2,5]{4,1,0,5,6,3,2:T(2,128)} %bitcast.95) | data formatting | bytes 122880 | tf_op jit(solution)/shard_map/transpose | solution.py:148
  43.5 0.1 copy.91
  43.6 0.8 reshape.291
  44.3 3.5 %all-to-all-start = ((f32[8,1,1920]{2,1,0:T(1,128)}), f32[8,1,1920]{2,1,0:T(1,128)S(1)}, u32[]{:S(2)}, u32[]{:S(2)}) async-start(f32[8,1,1920]{2,1,0:T(1,128)} %reshape.291), calls=%async_computation | async-start | bytes 122880 | tf_op jit(solution)/shard_map/all_to_all | solution.py:150
  47.9 4.1 %all-to-all-done = f32[8,1,1920]{2,1,0:T(1,128)S(1)} async-done(((f32[8,1,1920]{2,1,0:T(1,128)}), f32[8,1,1920]{2,1,0:T(1,128)S(1)}, u32[]{:S(2)}, u32[]{:S(2)}) %all-to-all-start) | async-done | bytes 61472 | tf_op jit(solution)/shard_map/all_to_all | solution.py:150
  51.9 0.5 broadcast.204
  52.5 0.8 reduce
  53.3 0.1 reshape.292
  53.4 1.6 %copy.59 = f32[64,1,3,2,4,2,5]{6,4,5,3,2,1,0:T(4,128)} copy(f32[64,1,3,2,4,2,5]{0,5,6,2,4,3,1:T(2,128)S(1)} %bitcast.103) | data formatting | bytes 122880 | tf_op jit(solution)/shard_map/reshape | solution.py:151
  55.0 3.8 %reshape.293 = f32[64,1,240]{2,1,0:T(1,128)} reshape(f32[64,1,3,2,2,4,5]{6,5,4,3,2,1,0:T(4,128)} %bitcast.96) | data formatting | bytes 122880
  58.8 18.3 %all-to-all-start.1 = ((f32[64,1,240]{2,1,0:T(1,128)}), f32[64,1,240]{2,1,0:T(1,128)S(1)}, u32[]{:S(2)}, u32[]{:S(2)}) async-start(f32[64,1,240]{2,1,0:T(1,128)} %reshape.293), calls=%async_computation.1 | async-start | bytes 131072 | tf_op jit(solution)/shard_map/all_to_all | solution.py:152
  77.1 0.2 mul.273
  77.4 0.1 copy.61
  77.4 2.6 %reshape.276 = f32[3,64,2,5,384]{4,3,2,1,0:T(8,128)} reshape(f32[3,640,384]{2,1,0:T(8,128)S(1)} %convert_multiply_fusion) | data formatting | bytes 5898240 | tf_op jit(solution)/shard_map/reshape | solution.py:156
  80.1 0.1 add_divide_fusion
  80.1 10.5 %all-to-all-done.1 = f32[64,1,240]{2,1,0:T(1,128)S(1)} async-done(((f32[64,1,240]{2,1,0:T(1,128)}), f32[64,1,240]{2,1,0:T(1,128)S(1)}, u32[]{:S(2)}, u32[]{:S(2)}) %all-to-all-start.1) | async-done | bytes 61472 | tf_op jit(solution)/shard_map/all_to_all | solution.py:152
  90.6 0.8 reduce.1
  91.4 1.8 %reshape.294 = f32[64,1,3,2,2,4,5]{6,5,4,3,2,1,0:T(4,128)S(1)} reshape(f32[64,240]{1,0:T(8,128)S(1)} %reduce.1) | data formatting | bytes 122880
  93.2 0.8 copy.60
  94.0 3.9 %fusion.20 = f32[8,3,384]{2,0,1:T(8,128)S(1)} fusion(f32[3,64,2,5,384]{4,3,2,1,0:T(8,128)} %reshape.276, f32[64,3,2,8,5]{0,3,4,2,1:T(8,128)S(1)} %bitcast.101, f32[64,2,5]{0,2,1:T(8,128)S(1)} %copy.61), kind=kOutput, calls=%fused_computation.16 | convolution fusion | flops 35404800 | bytes 3049984 | tf_op jit(solution)/shard_map/awblp,wabpn->lwn/dot_general | solution.py:158
  97.9 0.0 copy-done
  97.9 0.2 fusion.23
  98.1 0.2 convolution_bitcast_fusion
  98.2 4.9 %fusion.11 = f32[64,3,2,8,5]{0,3,4,2,1:T(8,128)S(1)} fusion(f32[8,3,384,1,1]{2,0,4,3,1:T(8,128)S(1)} %convolution_bitcast_fusion, f32[3,64,2,5,384]{4,3,2,1,0:T(8,128)} %reshape.276), kind=kOutput, calls=%fused_computation.13 | convolution fusion | flops 35389440 | bytes 3047424 | tf_op jit(solution)/shard_map/lwn,wabpn->awblp/dot_general | solution.py:162
  103.2 1.0 copy.65
  104.2 0.9 reshape.295
  105.2 18.6 %all_to_all.45 = f32[64,1,240]{2,1,0:T(1,128)S(1)} all-to-all(f32[64,1,240]{2,1,0:T(1,128)S(1)} %reshape.295), channel_id=1, replica_groups=mesh['lo'=64,'lc'=2,'lev'=4] {'lo'}, dimensions={0} | all-to-all | bytes 122880 | tf_op jit(solution)/shard_map/all_to_all | solution.py:164
  123.7 0.8 reduce.2
  124.5 0.7 reshape.296
  125.2 0.3 bitcast_bitcast_fusion
  125.5 0.9 copy.66
  126.4 0.8 reshape.297
  127.2 5.8 %all-to-all-start.3 = ((f32[8,1,1920]{2,1,0:T(1,128)}), f32[8,1,1920]{2,1,0:T(1,128)S(1)}, u32[]{:S(2)}, u32[]{:S(2)}) async-start(f32[8,1,1920]{2,1,0:T(1,128)} %reshape.297), calls=%async_computation.3 | async-start | bytes 122880 | tf_op jit(solution)/shard_map/all_to_all | solution.py:165
  133.1 4.9 %all-to-all-done.3 = f32[8,1,1920]{2,1,0:T(1,128)S(1)} async-done(((f32[8,1,1920]{2,1,0:T(1,128)}), f32[8,1,1920]{2,1,0:T(1,128)S(1)}, u32[]{:S(2)}, u32[]{:S(2)}) %all-to-all-start.3) | async-done | bytes 61472 | tf_op jit(solution)/shard_map/all_to_all | solution.py:165
  138.0 0.8 reduce.3
  138.8 0.1 reshape.298
  138.9 1.5 copy.68
  140.4 3.4 %reshape.283 = f32[2,2,2,5,384]{4,2,3,1,0:T(2,128)S(1)} reshape(f32[2,2,2,5,64,2,3]{6,5,4,2,3,1,0:T(2,128)S(1)} %copy.68) | data formatting | bytes 122880 | tf_op jit(solution)/shard_map/reshape | solution.py:167
  143.9 6.8 %fusion.4 = f32[2,5,2,2560]{3,1,2,0:T(8,128)S(1)} fusion(f32[1,2560,384]{2,1,0:T(8,128)} %bitcast.94, f32[1,2560,384]{2,1,0:T(8,128)} %bitcast.92, f32[2,2,2,5,384]{4,2,3,1,0:T(2,128)S(1)} %broadcast_multiply_fusion), kind=kOutput, calls=%fused_computation.7 | convolution fusion | flops 237895680 | bytes 8130560 | tf_op jit(solution)/shard_map/frlpm,rjm->fplj/dot_general | solution.py:168
  150.7 0.8 copy.70
  (18 shorter events, 0.2 us)
Async XLA Ops:
  0.0 97.9 %copy-start = (f32[8,8]{1,0:T(8,128)S(1)}, f32[8,8]{1,0:T(8,128)}, u32[]{:S(2)}) copy-start(f32[8,8]{1,0:T(8,128)} %param.13) | copy-start | bytes 772
  1.8 17.3 %collective-permute-start = (f32[2,4,2,2560]{3,1,0,2:T(4,128)}, f32[2,4,2,2560]{3,1,0,2:T(4,128)S(1)}, u32[]{:S(2)}, u32[]{:S(2)}) collective-permute-start(f32[2,4,2,2560]{3,1,0,2:T(4,128)} %get-tuple-element.5), channel_id=1, source_target_pairs={{0,4},{4,8},{8,12},{12,16},{16,20},{20,24},{24,28},{28,32},{32,36}... | collective-permute-start | bytes 491528 | tf_op jit(solution)/shard_map/ppermute | solution.py:23
  6.7 12.4 %collective-permute-start.1 = (f32[2,4,2,2560]{3,1,0,2:T(4,128)}, f32[2,4,2,2560]{3,1,0,2:T(4,128)}, u32[]{:S(2)}, u32[]{:S(2)}) collective-permute-start(f32[2,4,2,2560]{3,1,0,2:T(4,128)} %get-tuple-element.6), channel_id=1, source_target_pairs={{4,0},{8,4},{12,8},{16,12},{20,16},{24,20},{28,24},{32,28},{36,32}... | collective-permute-start | bytes 491528 | tf_op jit(solution)/shard_map/ppermute | solution.py:24
  12.7 4.0 %copy-start.1 = (bf16[3,640,384]{2,1,0:T(8,128)(2,1)S(1)}, bf16[3,640,384]{2,1,0:T(8,128)(2,1)}, u32[]{:S(2)}) copy-start(bf16[3,640,384]{2,1,0:T(8,128)(2,1)} %param.11) | copy-start | bytes 4423684
  16.7 0.9 copy-start.2
  16.7 0.9 copy-start.3
  35.2 12.7 %copy-start.6 = (f32[8]{0:T(128)S(1)}, f32[8]{0:T(128)}, u32[]{:S(2)}) copy-start(f32[8]{0:T(128)} %param.15) | copy-start | bytes 100
  40.4 36.7 %copy-start.4 = (f32[640]{0:T(1024)S(1)}, f32[640]{0:T(1024)}, u32[]{:S(2)}) copy-start(f32[640]{0:T(1024)} %param.12) | copy-start | bytes 7684
  44.3 7.6 %all-to-all-start = ((f32[8,1,1920]{2,1,0:T(1,128)}), f32[8,1,1920]{2,1,0:T(1,128)S(1)}, u32[]{:S(2)}, u32[]{:S(2)}) async-start(f32[8,1,1920]{2,1,0:T(1,128)} %reshape.291), calls=%async_computation | async-start | bytes 122880 | tf_op jit(solution)/shard_map/all_to_all | solution.py:150
  58.8 31.9 %all-to-all-start.1 = ((f32[64,1,240]{2,1,0:T(1,128)}), f32[64,1,240]{2,1,0:T(1,128)S(1)}, u32[]{:S(2)}, u32[]{:S(2)}) async-start(f32[64,1,240]{2,1,0:T(1,128)} %reshape.293), calls=%async_computation.1 | async-start | bytes 131072 | tf_op jit(solution)/shard_map/all_to_all | solution.py:152
  80.1 18.0 %copy-start.5 = (f32[8,8]{1,0:T(8,128)S(1)}, f32[8,8]{1,0:T(8,128)}, u32[]{:S(2)}) copy-start(f32[8,8]{1,0:T(8,128)} %param.14) | copy-start | bytes 772
  127.2 10.8 %all-to-all-start.3 = ((f32[8,1,1920]{2,1,0:T(1,128)}), f32[8,1,1920]{2,1,0:T(1,128)S(1)}, u32[]{:S(2)}, u32[]{:S(2)}) async-start(f32[8,1,1920]{2,1,0:T(1,128)} %reshape.297), calls=%async_computation.3 | async-start | bytes 122880 | tf_op jit(solution)/shard_map/all_to_all | solution.py:165

commit v4 on v3

--- a/solution.py
+++ b/solution.py
@@ -49,24 +49,26 @@
 
 
 def advect_kernel(padded_ref, row_ref, col_ref, out_ref, weight_ref, rolled_ref):
-    nfield = padded_ref.shape[1]
+    nfield, nrow = padded_ref.shape[1], padded_ref.shape[2]
     npoint, nlon = row_ref.shape[1], row_ref.shape[2]
+    tall = weight_ref.shape[1]
     dep_col = col_ref[0]
     for index, shift in enumerate(range(-5, 7)):
-        weight_ref[index] = tap_weight(dep_col, shift)
+        weight_ref[index, :npoint] = tap_weight(dep_col, shift)
     dep_row = row_ref[0]
+    row_weights = [tap_weight(dep_row, row_shift) for row_shift in range(-3, 5)]
     for field in range(nfield):
         block = padded_ref[0, field]
         for index, shift in enumerate(range(-5, 7)):
-            rolled_ref[index] = pltpu.roll(block, (-shift) % nlon, 1) if shift % nlon else block
+            rolled_ref[index, :nrow] = pltpu.roll(block, (-shift) % nlon, 1) if shift % nlon else block
         result = None
-        for row_shift in range(-3, 5):
+        for count, row_shift in enumerate(range(-3, 5)):
             first = 4 + row_shift
             inner = None
             for index in range(12):
-                term = weight_ref[index] * rolled_ref[index, first : first + npoint, :]
+                term = weight_ref[index] * rolled_ref[index, first : first + tall, :]
                 inner = term if inner is None else inner + term
-            term = tap_weight(dep_row, row_shift) * inner
+            term = row_weights[count] * inner[:npoint]
             result = term if result is None else result + term
         out_ref[0, field] = result
 
@@ -75,23 +77,19 @@
     nlev, nfield, nrow, nlon = padded.shape
     npoint = dep_row.shape[1]
     tall = -(-npoint // 8) * 8
-    padded = jnp.pad(padded, ((0, 0), (0, 0), (0, tall + 8 - nrow), (0, 0)))
-    dep_row = jnp.pad(dep_row, ((0, 0), (0, tall - npoint), (0, 0)))
-    dep_col = jnp.pad(dep_col, ((0, 0), (0, tall - npoint), (0, 0)))
-    out = pl.pallas_call(
+    return pl.pallas_call(
         advect_kernel,
         grid=(nlev,),
         in_specs=[
-            pl.BlockSpec((1, nfield, tall + 8, nlon), lambda l: (l, 0, 0, 0)),
-            pl.BlockSpec((1, tall, nlon), lambda l: (l, 0, 0)),
-            pl.BlockSpec((1, tall, nlon), lambda l: (l, 0, 0)),
+            pl.BlockSpec((1, nfield, nrow, nlon), lambda l: (l, 0, 0, 0)),
+            pl.BlockSpec((1, npoint, nlon), lambda l: (l, 0, 0)),
+            pl.BlockSpec((1, npoint, nlon), lambda l: (l, 0, 0)),
         ],
-        out_specs=pl.BlockSpec((1, nfield, tall, nlon), lambda l: (l, 0, 0, 0)),
-        out_shape=jax.ShapeDtypeStruct((nlev, nfield, tall, nlon), jnp.float32),
+        out_specs=pl.BlockSpec((1, nfield, npoint, nlon), lambda l: (l, 0, 0, 0)),
+        out_shape=jax.ShapeDtypeStruct((nlev, nfield, npoint, nlon), jnp.float32),
         scratch_shapes=[pltpu.VMEM((12, tall, nlon), jnp.float32), pltpu.VMEM((12, tall + 8, nlon), jnp.float32)],
         interpret=interpret,
     )(padded, dep_row, dep_col)
-    return out[:, :, :npoint]
 
 
 def split_factor(n):

time: 152 us -> 152 us (level)
    pad x3 -> x0, local copies, waits for them, and re-layouts: 2.24 us -> none  [the longest x1 0.88 us: advect_kernel_call(): padded = jnp.pad(padded, ((0, 0), (0, 0), (0, tall + 8 - nrow), (0, 0)))]
    transpose x0 -> x1, local copies, waits for them, and re-layouts: none -> 1.74 us  [per_device(): jnp.transpose(dep_col, (1, 0, 2))]
    unnamed x25 -> x19, local copies, waits for them, and re-layouts: 10.8 us -> 10 us
where the time goes in v4:
time: 152 us
  starting transfers between devices  37.7 us (25%)
  local copies, waits for them, and re-layouts  34.8 us (23%)
  matrix products  21.3 us (14%)
  waiting for transfers between devices  19.5 us (13%)
  blocking collectives  18.6 us (12%)
  other arithmetic  10.4 us (7%)
  Pallas kernels  9 us (6%)
    all_to_all x1, blocking collectives, per_device(): lax.all_to_all(staged, 'lo', split_axis=0, concat_axis=1, tiled=True)  18.6 us
    all_to_all x1, starting transfers between devices, per_device(): lax.all_to_all(staged, 'lo', split_axis=0, concat_axis=1, tiled=True)  18.3 us
    all_to_all x1, waiting for transfers between devices, per_device(): lax.all_to_all(staged, 'lo', split_axis=0, concat_axis=1, tiled=True)  10.5 us
    unnamed x19, local copies, waits for them, and re-layouts  10 us
    pallas_call x1, Pallas kernels, advect_kernel_call(): pl.pallas_call(advect_kernel, grid=(nlev,), in_specs=[pl.BlockSpec((1, nf...  9 us
    dot_general x1, matrix products, per_device(): jnp.einsum('frlpm,rjm->fplj', by_lat * doubling, table, precision=three_p...  6.81 us
    all_to_all x1, starting transfers between devices, per_device(): lax.all_to_all(staged, ('lc', 'lev'), split_axis=3, concat_axis=4, tiled=...  5.84 us
    dot_general x1, matrix products, per_device(): jnp.einsum('lfpj,rjm->mfrlp', advected, table, precision=three_pass)  5.4 us
  transfers between devices with their start and end apart: 5, of which 3 were waited for; matrix products, arithmetic and copies ran while one was open for 6% of the time, Pallas kernels for 0%

profile of v4, /device:TPU:1, one launch (start us, length us, event | category | flops | bytes accessed | tf_op | source)
XLA Modules:
  0.0 151.6 jit_solution(9055532267103977341)
XLA Ops:
  0.0 0.0 copy-start
  0.0 1.0 copy.51
  1.0 0.8 fusion.49
  1.8 4.9 %collective-permute-start = (f32[2,4,2,2560]{3,1,0,2:T(4,128)}, f32[2,4,2,2560]{3,1,0,2:T(4,128)S(1)}, u32[]{:S(2)}, u32[]{:S(2)}) collective-permute-start(f32[2,4,2,2560]{3,1,0,2:T(4,128)} %get-tuple-element.5), channel_id=1, source_target_pairs={{0,4},{4,8},{8,12},{12,16},{16,20},{20,24},{24,28},{28,32},{32,36}... | collective-permute-start | bytes 491528 | tf_op jit(solution)/shard_map/ppermute | solution.py:23
  6.7 5.1 %collective-permute-start.1 = (f32[2,4,2,2560]{3,1,0,2:T(4,128)}, f32[2,4,2,2560]{3,1,0,2:T(4,128)}, u32[]{:S(2)}, u32[]{:S(2)}) collective-permute-start(f32[2,4,2,2560]{3,1,0,2:T(4,128)} %get-tuple-element.6), channel_id=1, source_target_pairs={{4,0},{8,4},{12,8},{16,12},{20,16},{24,20},{28,24},{32,28},{36,32}... | collective-permute-start | bytes 491528 | tf_op jit(solution)/shard_map/ppermute | solution.py:24
  11.9 0.3 fusion.39
  12.2 0.1 fusion.42
  12.2 0.5 fusion.32
  12.7 1.7 %copy_bitcast_fusion = (s32[2,5,2560]{2,1,0:T(8,128)}, s32[2,5,2560]{2,1,0:T(8,128)}) fusion(s32[5,2,2560]{2,1,0:T(2,128)} %param.10, s32[5,2,2560]{2,1,0:T(2,128)} %param.9), kind=kLoop, calls=%fused_computation.22 | loop fusion | bytes 409600 | tf_op jit(solution)/shard_map/transpose | solution.py:138
  14.4 0.0 copy-start.1
  14.4 4.0 %multiply_subtract_fusion = (f32[64,40,384]{2,1,0:T(8,128)}, f32[64,40,384]{2,1,0:T(8,128)}) fusion(f32[40,384]{1,0:T(8,128)S(1)} %get-tuple-element.11, f32[64,384]{1,0:T(8,128)S(1)} %get-tuple-element.10, f32[40,384]{1,0:T(8,128)S(1)} %get-tuple-element.12, f32[64,384]{1,0:T(8,128)S(1)} %get-tuple-element.9), kind=kLoop, calls=%fused_computation.6 | loop fusion | flops 6881280 | bytes 8183808 | tf_op jit(solution)/shard_map/sub | solution.py:111
  18.5 0.0 copy-done.1
  18.5 0.2 convert_multiply_fusion
  18.7 0.0 collective-permute-done
  18.7 0.0 collective-permute-done.1
  18.7 1.9 %maximum_bitcast_fusion.padded_ref = f32[2,2,13,2560]{3,2,1,0:T(8,128)} fusion(f32[2,4,2,2560]{3,1,0,2:T(4,128)} %collective-permute-done.1, f32[2,5,2,2560]{3,1,0,2:T(8,128)S(1)} %copy.51, f32[2,4,2,2560]{3,1,0,2:T(4,128)S(1)} %collective-permute-done), kind=kLoop, calls=%fused_computation.20 | loop fusion | flops 266240 | bytes 1064960 | tf_op jit(solution)/shard_map/transpose | solution.py:136
  20.6 9.0 %shard_map.82 = f32[2,2,5,2560]{3,2,1,0:T(8,128)} custom-call(f32[2,2,13,2560]{3,2,1,0:T(8,128)} %maximum_bitcast_fusion.padded_ref, s32[2,5,2560]{2,1,0:T(8,128)} %get-tuple-element.14.row_ref, s32[2,5,2560]{2,1,0:T(8,128)} %get-tuple-element.13.col_ref), custom_call_target="tpu_custom_call" | custom-call | tf_op jit(solution)/shard_map/pallas_call | solution.py:80
  29.6 5.4 %fusion.17 = f32[384,2,2,2,5]{0,4,1,3,2:T(8,128)S(1)} fusion(f32[1,2560,384]{2,1,0:T(8,128)} %bitcast.91, f32[1,2560,384]{2,1,0:T(8,128)} %bitcast.89, f32[2,2,5,2560]{3,2,1,0:T(8,128)} %shard_map.82), kind=kOutput, calls=%fused_computation.15 | convolution fusion | flops 237911040 | bytes 8130560 | tf_op jit(solution)/shard_map/lfpj,rjm->mfrlp/dot_general | solution.py:144
  35.0 0.0 copy-start.4
  35.0 5.2 %reshape.277 = f32[64,2,3,2,2,2,5]{2,1,0,5,6,4,3:T(2,128)} reshape(f32[384,2,2,2,5]{0,3,4,2,1:T(2,128)S(1)} %copy.56) | data formatting | bytes 122880 | tf_op jit(solution)/shard_map/reshape | solution.py:145
  40.3 0.0 copy-start.2
  40.3 3.1 %copy.57 = f32[64,2,2,2,3,2,5]{0,3,2,1,6,5,4:T(2,128)S(1)} copy(f32[64,2,2,2,3,2,5]{4,1,0,5,6,3,2:T(2,128)} %bitcast.93) | data formatting | bytes 122880 | tf_op jit(solution)/shard_map/transpose | solution.py:146
  43.3 0.1 copy.89
  43.4 0.8 reshape.291
  44.2 3.5 %all-to-all-start = ((f32[8,1,1920]{2,1,0:T(1,128)}), f32[8,1,1920]{2,1,0:T(1,128)S(1)}, u32[]{:S(2)}, u32[]{:S(2)}) async-start(f32[8,1,1920]{2,1,0:T(1,128)} %reshape.291), calls=%async_computation | async-start | bytes 122880 | tf_op jit(solution)/shard_map/all_to_all | solution.py:148
  47.7 0.0 copy-done.4
  47.7 4.1 %all-to-all-done = f32[8,1,1920]{2,1,0:T(1,128)S(1)} async-done(((f32[8,1,1920]{2,1,0:T(1,128)}), f32[8,1,1920]{2,1,0:T(1,128)S(1)}, u32[]{:S(2)}, u32[]{:S(2)}) %all-to-all-start) | async-done | bytes 61472 | tf_op jit(solution)/shard_map/all_to_all | solution.py:148
  51.8 0.6 broadcast.198
  52.4 0.8 reduce
  53.2 0.1 reshape.292
  53.3 1.6 %copy.59 = f32[64,1,3,2,4,2,5]{6,4,5,3,2,1,0:T(4,128)} copy(f32[64,1,3,2,4,2,5]{0,5,6,2,4,3,1:T(2,128)S(1)} %bitcast.99) | data formatting | bytes 122880 | tf_op jit(solution)/shard_map/reshape | solution.py:149
  54.9 3.8 %reshape.293 = f32[64,1,240]{2,1,0:T(1,128)} reshape(f32[64,1,3,2,2,4,5]{6,5,4,3,2,1,0:T(4,128)} %bitcast.94) | data formatting | bytes 122880
  58.7 18.3 %all-to-all-start.1 = ((f32[64,1,240]{2,1,0:T(1,128)}), f32[64,1,240]{2,1,0:T(1,128)S(1)}, u32[]{:S(2)}, u32[]{:S(2)}) async-start(f32[64,1,240]{2,1,0:T(1,128)} %reshape.293), calls=%async_computation.1 | async-start | bytes 131072 | tf_op jit(solution)/shard_map/all_to_all | solution.py:150
  77.0 0.0 copy-done.2
  77.0 0.2 mul.273
  77.3 0.1 copy.61
  77.4 2.6 %reshape.276 = f32[3,64,2,5,384]{4,3,2,1,0:T(8,128)} reshape(f32[3,640,384]{2,1,0:T(8,128)S(1)} %convert_multiply_fusion) | data formatting | bytes 5898240 | tf_op jit(solution)/shard_map/reshape | solution.py:154
  80.0 0.1 add_divide_fusion
  80.1 10.5 %all-to-all-done.1 = f32[64,1,240]{2,1,0:T(1,128)S(1)} async-done(((f32[64,1,240]{2,1,0:T(1,128)}), f32[64,1,240]{2,1,0:T(1,128)S(1)}, u32[]{:S(2)}, u32[]{:S(2)}) %all-to-all-start.1) | async-done | bytes 61472 | tf_op jit(solution)/shard_map/all_to_all | solution.py:150
  90.5 0.8 reduce.1
  91.4 1.8 %reshape.294 = f32[64,1,3,2,2,4,5]{6,5,4,3,2,1,0:T(4,128)S(1)} reshape(f32[64,240]{1,0:T(8,128)S(1)} %reduce.1) | data formatting | bytes 122880
  93.2 0.8 copy.60
  94.0 3.9 %fusion.20 = f32[8,3,384]{2,0,1:T(8,128)S(1)} fusion(f32[3,64,2,5,384]{4,3,2,1,0:T(8,128)} %reshape.276, f32[64,3,2,8,5]{0,3,4,2,1:T(8,128)S(1)} %bitcast.97, f32[64,2,5]{0,2,1:T(8,128)S(1)} %copy.61), kind=kOutput, calls=%fused_computation.16 | convolution fusion | flops 35404800 | bytes 3049984 | tf_op jit(solution)/shard_map/awblp,wabpn->lwn/dot_general | solution.py:156
  97.8 0.0 copy-done
  97.8 0.2 fusion.23
  98.0 0.0 copy-done.3
  98.0 0.2 convolution_bitcast_fusion
  98.2 4.9 %fusion.11 = f32[64,3,2,8,5]{0,3,4,2,1:T(8,128)S(1)} fusion(f32[8,3,384,1,1]{2,0,4,3,1:T(8,128)S(1)} %convolution_bitcast_fusion, f32[3,64,2,5,384]{4,3,2,1,0:T(8,128)} %reshape.276), kind=kOutput, calls=%fused_computation.13 | convolution fusion | flops 35389440 | bytes 3047424 | tf_op jit(solution)/shard_map/lwn,wabpn->awblp/dot_general | solution.py:160
  103.2 1.0 copy.65
  104.2 0.9 reshape.295
  105.1 18.6 %all_to_all.45 = f32[64,1,240]{2,1,0:T(1,128)S(1)} all-to-all(f32[64,1,240]{2,1,0:T(1,128)S(1)} %reshape.295), channel_id=1, replica_groups=mesh['lo'=64,'lc'=2,'lev'=4] {'lo'}, dimensions={0} | all-to-all | bytes 122880 | tf_op jit(solution)/shard_map/all_to_all | solution.py:162
  123.7 0.8 reduce.2
  124.6 0.7 reshape.296
  125.2 0.3 bitcast_bitcast_fusion
  125.6 0.9 copy.66
  126.5 0.8 reshape.297
  127.2 5.8 %all-to-all-start.3 = ((f32[8,1,1920]{2,1,0:T(1,128)}), f32[8,1,1920]{2,1,0:T(1,128)S(1)}, u32[]{:S(2)}, u32[]{:S(2)}) async-start(f32[8,1,1920]{2,1,0:T(1,128)} %reshape.297), calls=%async_computation.3 | async-start | bytes 122880 | tf_op jit(solution)/shard_map/all_to_all | solution.py:163
  133.1 4.9 %all-to-all-done.3 = f32[8,1,1920]{2,1,0:T(1,128)S(1)} async-done(((f32[8,1,1920]{2,1,0:T(1,128)}), f32[8,1,1920]{2,1,0:T(1,128)S(1)}, u32[]{:S(2)}, u32[]{:S(2)}) %all-to-all-start.3) | async-done | bytes 61472 | tf_op jit(solution)/shard_map/all_to_all | solution.py:163
  138.0 0.8 reduce.3
  138.9 0.1 reshape.298
  139.0 1.5 copy.68
  140.5 3.4 %reshape.283 = f32[2,2,2,5,384]{4,2,3,1,0:T(2,128)S(1)} reshape(f32[2,2,2,5,64,2,3]{6,5,4,2,3,1,0:T(2,128)S(1)} %copy.68) | data formatting | bytes 122880 | tf_op jit(solution)/shard_map/reshape | solution.py:165
  143.9 6.8 %fusion.4 = f32[2,5,2,2560]{3,1,2,0:T(8,128)S(1)} fusion(f32[1,2560,384]{2,1,0:T(8,128)} %bitcast.92, f32[1,2560,384]{2,1,0:T(8,128)} %bitcast.90, f32[2,2,2,5,384]{4,2,3,1,0:T(2,128)S(1)} %broadcast_multiply_fusion), kind=kOutput, calls=%fused_computation.7 | convolution fusion | flops 237895680 | bytes 8130560 | tf_op jit(solution)/shard_map/frlpm,rjm->fplj/dot_general | solution.py:166
  150.8 0.8 copy.70
  (10 shorter events, 0.1 us)
Async XLA Ops:
  0.0 97.8 %copy-start = (f32[8,8]{1,0:T(8,128)S(1)}, f32[8,8]{1,0:T(8,128)}, u32[]{:S(2)}) copy-start(f32[8,8]{1,0:T(8,128)} %param.13) | copy-start | bytes 772
  1.8 16.9 %collective-permute-start = (f32[2,4,2,2560]{3,1,0,2:T(4,128)}, f32[2,4,2,2560]{3,1,0,2:T(4,128)S(1)}, u32[]{:S(2)}, u32[]{:S(2)}) collective-permute-start(f32[2,4,2,2560]{3,1,0,2:T(4,128)} %get-tuple-element.5), channel_id=1, source_target_pairs={{0,4},{4,8},{8,12},{12,16},{16,20},{20,24},{24,28},{28,32},{32,36}... | collective-permute-start | bytes 491528 | tf_op jit(solution)/shard_map/ppermute | solution.py:23
  6.7 12.0 %collective-permute-start.1 = (f32[2,4,2,2560]{3,1,0,2:T(4,128)}, f32[2,4,2,2560]{3,1,0,2:T(4,128)}, u32[]{:S(2)}, u32[]{:S(2)}) collective-permute-start(f32[2,4,2,2560]{3,1,0,2:T(4,128)} %get-tuple-element.6), channel_id=1, source_target_pairs={{4,0},{8,4},{12,8},{16,12},{20,16},{24,20},{28,24},{32,28},{36,32}... | collective-permute-start | bytes 491528 | tf_op jit(solution)/shard_map/ppermute | solution.py:24
  14.4 4.0 %copy-start.1 = (bf16[3,640,384]{2,1,0:T(8,128)(2,1)S(1)}, bf16[3,640,384]{2,1,0:T(8,128)(2,1)}, u32[]{:S(2)}) copy-start(bf16[3,640,384]{2,1,0:T(8,128)(2,1)} %param.11) | copy-start | bytes 4423684
  35.0 12.7 %copy-start.4 = (f32[8]{0:T(128)S(1)}, f32[8]{0:T(128)}, u32[]{:S(2)}) copy-start(f32[8]{0:T(128)} %param.15) | copy-start | bytes 100
  40.3 36.8 %copy-start.2 = (f32[640]{0:T(1024)S(1)}, f32[640]{0:T(1024)}, u32[]{:S(2)}) copy-start(f32[640]{0:T(1024)} %param.12) | copy-start | bytes 7684
  44.2 7.6 %all-to-all-start = ((f32[8,1,1920]{2,1,0:T(1,128)}), f32[8,1,1920]{2,1,0:T(1,128)S(1)}, u32[]{:S(2)}, u32[]{:S(2)}) async-start(f32[8,1,1920]{2,1,0:T(1,128)} %reshape.291), calls=%async_computation | async-start | bytes 122880 | tf_op jit(solution)/shard_map/all_to_all | solution.py:148
  58.7 31.9 %all-to-all-start.1 = ((f32[64,1,240]{2,1,0:T(1,128)}), f32[64,1,240]{2,1,0:T(1,128)S(1)}, u32[]{:S(2)}, u32[]{:S(2)}) async-start(f32[64,1,240]{2,1,0:T(1,128)} %reshape.293), calls=%async_computation.1 | async-start | bytes 131072 | tf_op jit(solution)/shard_map/all_to_all | solution.py:150
  80.0 18.0 %copy-start.3 = (f32[8,8]{1,0:T(8,128)S(1)}, f32[8,8]{1,0:T(8,128)}, u32[]{:S(2)}) copy-start(f32[8,8]{1,0:T(8,128)} %param.14) | copy-start | bytes 772
  127.2 10.8 %all-to-all-start.3 = ((f32[8,1,1920]{2,1,0:T(1,128)}), f32[8,1,1920]{2,1,0:T(1,128)S(1)}, u32[]{:S(2)}, u32[]{:S(2)}) async-start(f32[8,1,1920]{2,1,0:T(1,128)} %reshape.297), calls=%async_computation.3 | async-start | bytes 122880 | tf_op jit(solution)/shard_map/all_to_all | solution.py:163
